TPU v7x, 128 devices: a whole 4x4x4 slice. The times are simulated.
128 devices in a mesh: dp: 2 (over x_hi), pipe: 4 (over z), tensor: 16 (over y, x_lo, core).
Axes of the slice: x: 4 (x_hi: 2, x_lo: 2; x = x_hi * 2 + x_lo), y: 4, z: 4, core: 2. Of those that a mesh axis runs over, the one named last changes fastest.
Arguments:
- tokens: bfloat16 [2, 4, 2048, 4096], P('dp', 'pipe', 'tensor'), may hold values from -6 to 6
- norm_gain: float32 [4, 4096], P('pipe'), may hold values from 0.25 to 1.75
- query_weight: bfloat16 [4, 4096, 6144], P('pipe', None, 'tensor'), may hold values from -5.625 to 5.625
- kv_weight: bfloat16 [4, 4096, 2048], P('pipe'), may hold values from -0.09375 to 0.09375
- out_weight: bfloat16 [4, 6144, 4096], P('pipe', 'tensor'), may hold values from -0.75 to 0.75
Outputs:
- next_input: bfloat16 [2, 4, 2048, 4096], P('dp', 'pipe', 'tensor')
- max_logits: float32 [4, 48], P('pipe', 'tensor')
All inputs are finite; a program needn't handle non-finite values.
Results may differ from a plain program's by a relative error of at most 0.018.
The roundings to bfloat16 on the way count: a program that leaves them out, or rounds other values in their place, can miss the bound.
Values may be sent and summed in bfloat16 or wider, within the bound.
No kernel may reach another device: no remote copies, remote signals or barrier semaphores. Data moves between devices by JAX's collectives and lax.ppermute only.
A program may use at most 128 MiB of HBM per device.

v0:
```python
import math

import jax
import jax.numpy as jnp
from jax import lax
from jax.sharding import PartitionSpec as P

HD = 128
GROUP = 6


def from_behind(block, axis, distance):
    devices = range(lax.axis_size(axis))
    route = [((i - distance) % len(devices), i) for i in devices]
    return lax.ppermute(block, axis, route)


def on_device(tokens, norm_gain, query_weight, kv_weight, out_weight):
    inputs = tokens[0, 0]
    wide_in = inputs.astype(jnp.float32)
    normed = (
        wide_in
        * lax.rsqrt(jnp.mean(wide_in * wide_in, axis=1, keepdims=True) + 1e-05)
        * norm_gain[0][None, :]
    ).astype(jnp.bfloat16)
    query_local = query_weight[0]
    heads_dev = query_local.shape[1] // HD
    kv_dev = max(1, heads_dev // GROUP)
    kv_cols = kv_dev * 2 * HD
    query_cols = heads_dev * HD
    tensor_id = lax.axis_index("tensor")
    kv_start = tensor_id * heads_dev // GROUP
    kv_local = lax.dynamic_slice_in_dim(kv_weight[0], kv_start * 2 * HD, kv_cols, 1)
    joined = jnp.concatenate([query_local, kv_local], 1)
    projected = jnp.dot(
        lax.all_gather(normed, "tensor", axis=0, tiled=True),
        joined,
        preferred_element_type=jnp.float32,
    ).astype(jnp.bfloat16)
    queries = projected[:, :query_cols]
    keyvals = projected[:, query_cols:]
    seq_len = queries.shape[0]
    group_loc = heads_dev // kv_dev
    query_heads = queries.reshape(seq_len, kv_dev, group_loc, HD)
    kv_heads = keyvals.reshape(seq_len, kv_dev, 2, HD)
    key_heads = kv_heads[:, :, 0]
    value_heads = kv_heads[:, :, 1]
    block_rows = min(512, seq_len)
    score_scale = 1.0 / math.sqrt(HD)

    def attend(row_start):
        query_block = lax.dynamic_slice_in_dim(query_heads, row_start, block_rows, 0)
        scores = (
            jnp.einsum("qkgd,skd->kgqs", query_block, key_heads, preferred_element_type=jnp.float32)
            * score_scale
        )
        row_ids = row_start + jnp.arange(block_rows)
        col_ids = jnp.arange(seq_len)
        allowed = col_ids[None, :] <= row_ids[:, None]
        scores = jnp.where(allowed, scores, -jnp.inf)
        row_max = jnp.max(scores, axis=3, keepdims=True)
        expw = jnp.exp(scores - row_max)
        row_sum = jnp.sum(expw, axis=3, keepdims=True)
        blended = jnp.einsum(
            "kgqs,skd->qkgd",
            expw.astype(jnp.bfloat16),
            value_heads,
            preferred_element_type=jnp.float32,
        )
        blended = blended / jnp.transpose(row_sum, (2, 0, 1, 3))
        return (blended.astype(jnp.bfloat16), jnp.max(row_max[..., 0], axis=2))

    starts = jnp.arange(seq_len // block_rows) * block_rows
    outputs, head_peaks = lax.map(attend, starts)
    attended = outputs.reshape(seq_len, query_cols)
    peaks_local = jnp.max(head_peaks, axis=0)
    out_local = out_weight[0]
    summed = lax.psum_scatter(
        jnp.dot(attended, out_local, preferred_element_type=jnp.float32).astype(jnp.bfloat16),
        "tensor",
        scatter_dimension=0,
        tiled=True,
    ).astype(jnp.float32)
    result = (wide_in + summed).astype(jnp.bfloat16)
    peak_all = lax.pmax(peaks_local, "dp")
    passed = from_behind(result, "pipe", 1)
    return (passed[None, None], peak_all)


def solution(mesh):
    placed = (
        P("dp", "pipe", "tensor", None),
        P("pipe", None),
        P("pipe", None, "tensor"),
        P("pipe", None, None),
        P("pipe", "tensor", None),
    )
    return jax.shard_map(
        on_device,
        mesh=mesh,
        in_specs=placed,
        out_specs=(P("dp", "pipe", "tensor", None), P("pipe", "tensor")),
        check_vma=False,
    )
```

profile of v0, /device:TPU:0, one launch (start us, length us, event | category | flops | bytes accessed | tf_op | source)
XLA Modules:
  0.0 436.7 jit_solution(194145111903713398)
XLA Ops:
  7.2 0.0 copy-start
  7.2 0.0 all-gather.2.cloned.1.call-start
  7.2 1.7 fusion.39
  8.9 2.5 fusion.41
  11.4 0.0 all-gather.2.cloned.1.call-update
  11.5 0.0 reduce-scatter.2.cloned.1.call-start
  11.6 3.0 dynamic-slice_bitcast_fusion
  14.6 91.0 %all-gather.2.cloned.1.call-done = bf16[2048,4096]{1,0:T(8,128)(2,1)} async-done(((bf16[128,4096]{1,0:T(8,128)(2,1)}), bf16[2048,4096]{1,0:T(8,128)(2,1)}) %all-gather.2.cloned.1.call-update) | async-done | bytes 16777232 | tf_op jit(solution)/shard_map/all_gather | solution.py:36
  105.6 17.3 %fusion.35 = bf16[2048,640]{0,1:T(8,128)(2,1)} fusion(bf16[2048,4096]{1,0:T(8,128)(2,1)} %all-gather.2.cloned.1.call-done, bf16[4096,256]{1,0:T(8,128)(2,1)} %dynamic-slice_bitcast_fusion, bf16[4096,384]{1,0:T(8,128)(2,1)} %bitcast.140), kind=kOutput, calls=%fused_computation.30 | convolution fusion | flops 10749214720 | bytes 24641536 | tf_op jit(solution)/shard_map/dot_general | solution.py:35
  122.9 0.0 slice-start
  122.9 2.8 slice.16
  125.7 0.0 slice-done
  125.7 1.0 fusion.44
  126.8 2.1 copy.15
  128.8 2.0 copy.16
  130.9 67.5 %while.12 = (s32[]{:T(128)}, bf16[4,512,1,3,128]{4,1,3,2,0:T(8,128)(2,1)}, f32[4,1,3]{2,1,0:T(1,128)S(1)}, s32[4]{0:T(128)S(1)}, bf16[2048,1,3,128]{0,3,2,1:T(8,...) while((s32[]{:T(128)}, ...), condition=%wide.region_5.6_spmd, body=%wide.region_1.5_spmd.sunk | while | flops 1649800704 | bytes 45911748 | solution.py:74
  130.9 0.6 dynamic_slice.24
  133.4 0.6 iota_add_fusion.2
  134.0 0.7 iota_compare_fusion.2
  134.7 4.7 %fusion.54 = (f32[3,512]{1,0:T(4,128)S(1)}, f32[512,3,2048]{2,0,1:T(8,128)S(1)}) fusion(pred[512,2048]{1,0:T(8,128)(4,1)S(1)} %iota_compare_fusion.2, bf16[2048,1,128]{2,0,1:T(8,128)(2,1)} %get-tuple-element.152, bf16[2048,1,3,128]{0,3,2,1:T(8,128)(2,1)} %get-tuple-element.151, s32[]{:T(128)S(6)} %select_n.46), kind=kOutput, calls=%fused_computation.5.clone.1 | convolution fusion | flops 814742016 | bytes 14555140 | tf_op jit(solution)/shard_map/while/body/eval_jaxpr/qkgd,skd->kgqs/dot_general | solution.py:54
  139.4 0.0 copy-start.1
  139.4 4.1 fusion.55
  143.5 0.0 copy-done.1
  143.5 4.2 fusion.56
  147.8 0.6 dynamic_slice.24
  150.3 0.6 iota_add_fusion.2
  150.9 0.7 iota_compare_fusion.2
  151.6 4.7 %fusion.54 = (f32[3,512]{1,0:T(4,128)S(1)}, f32[512,3,2048]{2,0,1:T(8,128)S(1)}) fusion(pred[512,2048]{1,0:T(8,128)(4,1)S(1)} %iota_compare_fusion.2, bf16[2048,1,128]{2,0,1:T(8,128)(2,1)} %get-tuple-element.152, bf16[2048,1,3,128]{0,3,2,1:T(8,128)(2,1)} %get-tuple-element.151, s32[]{:T(128)S(6)} %select_n.46), kind=kOutput, calls=%fused_computation.5.clone.1 | convolution fusion | flops 814742016 | bytes 14555140 | tf_op jit(solution)/shard_map/while/body/eval_jaxpr/qkgd,skd->kgqs/dot_general | solution.py:54
  156.3 0.0 copy-start.1
  156.3 4.1 fusion.55
  160.4 0.0 copy-done.1
  160.4 4.2 fusion.56
  164.6 0.6 dynamic_slice.24
  167.2 0.6 iota_add_fusion.2
  167.8 0.7 iota_compare_fusion.2
  168.5 4.7 %fusion.54 = (f32[3,512]{1,0:T(4,128)S(1)}, f32[512,3,2048]{2,0,1:T(8,128)S(1)}) fusion(pred[512,2048]{1,0:T(8,128)(4,1)S(1)} %iota_compare_fusion.2, bf16[2048,1,128]{2,0,1:T(8,128)(2,1)} %get-tuple-element.152, bf16[2048,1,3,128]{0,3,2,1:T(8,128)(2,1)} %get-tuple-element.151, s32[]{:T(128)S(6)} %select_n.46), kind=kOutput, calls=%fused_computation.5.clone.1 | convolution fusion | flops 814742016 | bytes 14555140 | tf_op jit(solution)/shard_map/while/body/eval_jaxpr/qkgd,skd->kgqs/dot_general | solution.py:54
  173.2 0.0 copy-start.1
  173.2 4.1 fusion.55
  177.3 0.0 copy-done.1
  177.3 4.2 fusion.56
  181.5 0.6 dynamic_slice.24
  184.1 0.6 iota_add_fusion.2
  184.7 0.7 iota_compare_fusion.2
  185.4 4.6 %fusion.54 = (f32[3,512]{1,0:T(4,128)S(1)}, f32[512,3,2048]{2,0,1:T(8,128)S(1)}) fusion(pred[512,2048]{1,0:T(8,128)(4,1)S(1)} %iota_compare_fusion.2, bf16[2048,1,128]{2,0,1:T(8,128)(2,1)} %get-tuple-element.152, bf16[2048,1,3,128]{0,3,2,1:T(8,128)(2,1)} %get-tuple-element.151, s32[]{:T(128)S(6)} %select_n.46), kind=kOutput, calls=%fused_computation.5.clone.1 | convolution fusion | flops 814742016 | bytes 14555140 | tf_op jit(solution)/shard_map/while/body/eval_jaxpr/qkgd,skd->kgqs/dot_general | solution.py:54
  190.0 0.0 copy-start.1
  190.0 4.1 fusion.55
  194.2 0.0 copy-done.1
  194.2 4.2 fusion.56
  198.4 3.9 copy.13
  202.3 1.8 copy.17
  204.1 0.0 copy-done
  204.1 12.4 %convolution_convert_fusion = bf16[2048,4096]{1,0:T(8,128)(2,1)} fusion(bf16[2048,384]{0,1:T(8,128)(2,1)S(1)} %bitcast.134, bf16[1,384,4096]{2,1,0:T(8,128)(2,1)S(1)} %copy-done), kind=kOutput, calls=%fused_computation.25 | convolution fusion | flops 6450839552 | bytes 21495808 | tf_op jit(solution)/shard_map/dot_general | solution.py:79
  216.5 0.0 reduce-scatter.2.cloned.1.call-update
  216.6 183.4 %reduce-scatter.2.cloned.1.call-done = bf16[128,4096]{1,0:T(8,128)(2,1)} async-done(((bf16[2048,4096]{1,0:T(8,128)(2,1)}), bf16[128,4096]{1,0:T(8,128)(2,1)}) %reduce-scatter.2.cloned.1.call-update) | async-done | bytes 1048592 | tf_op jit(solution)/shard_map/reduce_scatter | solution.py:78
  399.9 2.8 fusion.42
  402.7 1.6 collective-permute-start
  404.3 6.9 %pmax.7 = f32[1,3]{1,0:T(1,128)} all-reduce(f32[1,3]{1,0:T(1,128)S(1)} %bitcast.139), channel_id=1, replica_groups=mesh['dp'=2,'pipe'=4,'tensor'=16] {'dp'}, use_global_device_ids=true, to_apply=%region_8.9 | all-reduce | flops 3 | bytes 24 | tf_op jit(solution)/shard_map/pmax | solution.py:85
  411.2 16.3 %collective-permute-done = bf16[128,4096]{1,0:T(8,128)(2,1)} collective-permute-done((bf16[128,4096]{1,0:T(8,128)(2,1)}, bf16[128,4096]{1,0:T(8,128)(2,1)}, u32[]{:S(2)}, u32[]{:S(2)}) %collective-permute-start) | collective-permute-done | bytes 1048608 | tf_op jit(solution)/shard_map/ppermute | solution.py:15
  427.6 2.3 copy.30
  (9 shorter events, 0.1 us)
Async XLA Ops:
  7.2 197.0 %copy-start = (bf16[1,384,4096]{2,1,0:T(8,128)(2,1)S(1)}, bf16[1,384,4096]{2,1,0:T(8,128)(2,1)}, u32[]{:S(2)}) copy-start(bf16[1,384,4096]{2,1,0:T(8,128)(2,1)} %param.11) | copy-start | bytes 9437188
  7.2 98.5 %all-gather.2.cloned.1.call-start = ((), (), s32[]{:S(2)}) async-start(), calls=%async_computation.1 | async-start | bytes 17825792 | tf_op jit(solution)/shard_map/all_gather | solution.py:36
  11.5 388.5 %reduce-scatter.2.cloned.1.call-start = ((), (), s32[]{:S(2)}) async-start(), calls=%async_computation.2 | async-start | bytes 17825792 | tf_op jit(solution)/shard_map/reduce_scatter | solution.py:78
  122.9 2.8 slice-start
  139.4 4.1 copy-start.1
  156.3 4.1 copy-start.1
  173.2 4.1 copy-start.1
  190.0 4.1 copy-start.1
  402.7 24.9 %collective-permute-start = (bf16[128,4096]{1,0:T(8,128)(2,1)}, bf16[128,4096]{1,0:T(8,128)(2,1)}, u32[]{:S(2)}, u32[]{:S(2)}) collective-permute-start(bf16[128,4096]{1,0:T(8,128)(2,1)} %fusion.42), channel_id=1, source_target_pairs={{48,0},{0,16},{16,32},{32,48},{49,1},{1,17},{17,33},{33,49},{50,2}... | collective-permute-start | bytes 3145736 | tf_op jit(solution)/shard_map/ppermute | solution.py:15
Sparse Core Ops, SparseCore 0:
  11.6 94.0 all-gather.1
  216.7 183.2 reduce-scatter.1
where the time goes:
time: 437 us
  waiting for transfers between devices  291 us (67%)
  matrix products  65.3 us (15%)
  other arithmetic  28.6 us (7%)
  local copies, waits for them, and re-layouts  21.4 us (5%)
  between operations  14.1 us (3%)
  loops' own time  7.95 us (2%)
  blocking collectives  6.93 us (2%)
    reduce_scatter x1, waiting for transfers between devices, on_device(): lax.psum_scatter(jnp.dot(attended, out_local, preferred_element_type=jnp....  183 us
    all_gather x1, waiting for transfers between devices, on_device(): lax.all_gather(normed, 'tensor', axis=0, tiled=True)  91 us
    dot_general x4, matrix products, attend(): jnp.einsum('qkgd,skd->kgqs', query_block, key_heads, preferred_element_ty...  18.7 us
    dot_general x1, matrix products, on_device(): jnp.dot(lax.all_gather(normed, 'tensor', axis=0, tiled=True), joined, pre...  17.3 us
    dot_general x4, matrix products, attend(): jnp.einsum('kgqs,skd->qkgd', expw.astype(jnp.bfloat16), value_heads, pref...  16.9 us
    reduce_max x4, other arithmetic, attend(): return (blended.astype(jnp.bfloat16), jnp.max(row_max[..., 0], axis=2))  16.4 us
    ppermute x1, waiting for transfers between devices, from_behind(): return lax.ppermute(block, axis, route)  16.3 us
    dot_general x1, matrix products, on_device(): jnp.dot(attended, out_local, preferred_element_type=jnp.float32)  12.4 us
  transfers between devices with their start and end apart: 3, of which 3 were waited for; matrix products, arithmetic and copies ran while one was open for 1% of the time, Pallas kernels for 0%

commit v1 on v0

--- a/solution.py
+++ b/solution.py
@@ -7,6 +7,7 @@
 
 HD = 128
 GROUP = 6
+N_BLOCKS = 4
 
 
 def from_behind(block, axis, distance):
@@ -28,6 +29,7 @@
     kv_dev = max(1, heads_dev // GROUP)
     kv_cols = kv_dev * 2 * HD
     query_cols = heads_dev * HD
+    n_tensor = lax.axis_size("tensor")
     tensor_id = lax.axis_index("tensor")
     kv_start = tensor_id * heads_dev // GROUP
     kv_local = lax.dynamic_slice_in_dim(kv_weight[0], kv_start * 2 * HD, kv_cols, 1)
@@ -40,22 +42,30 @@
     queries = projected[:, :query_cols]
     keyvals = projected[:, query_cols:]
     seq_len = queries.shape[0]
+    local_rows = inputs.shape[0]
     group_loc = heads_dev // kv_dev
     query_heads = queries.reshape(seq_len, kv_dev, group_loc, HD)
     kv_heads = keyvals.reshape(seq_len, kv_dev, 2, HD)
     key_heads = kv_heads[:, :, 0]
     value_heads = kv_heads[:, :, 1]
-    block_rows = min(512, seq_len)
     score_scale = 1.0 / math.sqrt(HD)
-
-    def attend(row_start):
-        query_block = lax.dynamic_slice_in_dim(query_heads, row_start, block_rows, 0)
+    out_local = out_weight[0]
+    sub = local_rows // N_BLOCKS
+    block_rows = n_tensor * sub
+    col_ids = jnp.arange(seq_len)
+    pieces = []
+    peaks = []
+    for b in range(N_BLOCKS):
+        query_block = query_heads.reshape(n_tensor, local_rows, kv_dev, group_loc, HD)[
+            :, b * sub : (b + 1) * sub
+        ].reshape(block_rows, kv_dev, group_loc, HD)
+        row_ids = (
+            jnp.arange(n_tensor)[:, None] * local_rows + b * sub + jnp.arange(sub)[None, :]
+        ).reshape(block_rows)
         scores = (
             jnp.einsum("qkgd,skd->kgqs", query_block, key_heads, preferred_element_type=jnp.float32)
             * score_scale
         )
-        row_ids = row_start + jnp.arange(block_rows)
-        col_ids = jnp.arange(seq_len)
         allowed = col_ids[None, :] <= row_ids[:, None]
         scores = jnp.where(allowed, scores, -jnp.inf)
         row_max = jnp.max(scores, axis=3, keepdims=True)
@@ -68,22 +78,15 @@
             preferred_element_type=jnp.float32,
         )
         blended = blended / jnp.transpose(row_sum, (2, 0, 1, 3))
-        return (blended.astype(jnp.bfloat16), jnp.max(row_max[..., 0], axis=2))
-
-    starts = jnp.arange(seq_len // block_rows) * block_rows
-    outputs, head_peaks = lax.map(attend, starts)
-    attended = outputs.reshape(seq_len, query_cols)
-    peaks_local = jnp.max(head_peaks, axis=0)
-    out_local = out_weight[0]
-    summed = lax.psum_scatter(
-        jnp.dot(attended, out_local, preferred_element_type=jnp.float32).astype(jnp.bfloat16),
-        "tensor",
-        scatter_dimension=0,
-        tiled=True,
-    ).astype(jnp.float32)
-    result = (wide_in + summed).astype(jnp.bfloat16)
-    peak_all = lax.pmax(peaks_local, "dp")
-    passed = from_behind(result, "pipe", 1)
+        attended = blended.astype(jnp.bfloat16).reshape(block_rows, query_cols)
+        peaks.append(jnp.max(row_max[..., 0], axis=2))
+        partial = jnp.dot(attended, out_local, preferred_element_type=jnp.float32).astype(jnp.bfloat16)
+        summed = lax.psum_scatter(partial, "tensor", scatter_dimension=0, tiled=True).astype(jnp.float32)
+        result = (wide_in[b * sub : (b + 1) * sub] + summed).astype(jnp.bfloat16)
+        pieces.append(from_behind(result, "pipe", 1))
+    peaks_local = jnp.max(jnp.stack(peaks), axis=0)
+    peak_all = jnp.maximum(peaks_local, from_behind(peaks_local, "dp", 1))
+    passed = jnp.concatenate(pieces, 0)
     return (passed[None, None], peak_all)
 
 

time: 437 us -> 487 us (1.11)
  waiting for transfers between devices: 291 us -> 326 us
  matrix products: 65.3 us -> 76.8 us
  other arithmetic: 28.6 us -> 37 us
  loops' own time: 7.95 us -> 0 us
  blocking collectives: 6.93 us -> 0 us
  starting transfers between devices: 1.63 us -> 8.08 us
    reduce_scatter x1 -> x4, waiting for transfers between devices: 183 us -> 223 us  [on_device(): lax.psum_scatter(partial, 'tensor', scatter_dimension=0, tiled=True)]
    slice x2 -> x5, local copies, waits for them, and re-layouts: 3.86 us -> 13.4 us  [on_device(): query_heads.reshape(n_tensor, local_rows, kv_dev, group_loc, HD)]
    another operation x1 -> x0, loops' own time: 7.95 us -> none  [on_device(): outputs, head_peaks = lax.map(attend, starts)]
    pmax x1 -> x0, blocking collectives: 6.93 us -> none  [on_device(): peak_all = lax.pmax(peaks_local, 'dp')]
    dot_general x8, matrix products: 35.6 us -> 42 us  [the longest x4 26.9 us: on_device(): jnp.einsum('kgqs,skd->qkgd', expw.astype(jnp.bfloat16), value_heads, pref...]
    unnamed x6 -> x32, local copies, waits for them, and re-layouts: 8.23 us -> 1.97 us
    ppermute x1 -> x5, starting transfers between devices: 1.55 us -> 7.7 us  [from_behind(): return lax.ppermute(block, axis, route)]
    dot_general x1 -> x4, matrix products: 12.4 us -> 17.4 us  [on_device(): jnp.dot(attended, out_local, preferred_element_type=jnp.float32)]
  transfers between devices with their start and end apart: 3 -> 10, of which waited for: 3 -> 9; matrix products, arithmetic and copies ran while one was open for 1% -> 15% of each run, Pallas kernels for 0% -> 0%
where the time goes in v1:
time: 487 us; the launch traced here: 484 us
  waiting for transfers between devices  326 us (67%)
  matrix products  76.8 us (16%)
  other arithmetic  37 us (8%)
  local copies, waits for them, and re-layouts  21 us (4%)
  between operations  14.2 us (3%)
  starting transfers between devices  8.08 us (2%)
    reduce_scatter x4, waiting for transfers between devices, on_device(): lax.psum_scatter(partial, 'tensor', scatter_dimension=0, tiled=True)  223 us
    all_gather x1, waiting for transfers between devices, on_device(): lax.all_gather(normed, 'tensor', axis=0, tiled=True)  87.1 us
    dot_general x4, matrix products, on_device(): jnp.einsum('kgqs,skd->qkgd', expw.astype(jnp.bfloat16), value_heads, pref...  26.9 us
    reduce_max x2, other arithmetic, on_device(): peaks.append(jnp.max(row_max[..., 0], axis=2))  18.8 us
    dot_general x1, matrix products, on_device(): jnp.dot(lax.all_gather(normed, 'tensor', axis=0, tiled=True), joined, pre...  17.4 us
    dot_general x4, matrix products, on_device(): jnp.dot(attended, out_local, preferred_element_type=jnp.float32)  17.4 us
    ppermute x5, waiting for transfers between devices, from_behind(): return lax.ppermute(block, axis, route)  16 us
    dot_general x4, matrix products, on_device(): jnp.einsum('qkgd,skd->kgqs', query_block, key_heads, preferred_element_ty...  15.1 us
  transfers between devices with their start and end apart: 10, of which 9 were waited for; matrix products, arithmetic and copies ran while one was open for 15% of the time, Pallas kernels for 0%

profile of v1, /device:TPU:0, one launch (start us, length us, event | category | flops | bytes accessed | tf_op | source)
XLA Modules:
  0.0 483.6 jit_solution(12084207283906105252)
XLA Ops:
  7.2 0.0 all-gather.2.cloned.1.call-start
  7.2 1.7 fusion.43
  8.9 2.6 fusion.45
  11.5 0.0 reduce-scatter.5.cloned.1.call-start
  11.6 0.1 iota_add_fusion.3
  11.6 0.1 add.145
  11.7 0.1 iota_add_fusion.2
  11.8 0.1 add.151
  11.9 1.8 iota_compare_fusion.3
  13.7 1.8 iota_compare_fusion.2
  15.5 3.0 dynamic-slice_bitcast_fusion
  18.5 87.1 %all-gather.2.cloned.1.call-done = bf16[2048,4096]{1,0:T(8,128)(2,1)} async-done(((bf16[128,4096]{1,0:T(8,128)(2,1)}), bf16[2048,4096]{1,0:T(8,128)(2,1)}) %all-gather.2.cloned.1.call-update) | async-done | bytes 16777232 | tf_op jit(solution)/shard_map/all_gather | solution.py:38
  105.7 17.4 %fusion.36 = bf16[2048,640]{0,1:T(8,128)(2,1)} fusion(bf16[2048,4096]{1,0:T(8,128)(2,1)} %all-gather.2.cloned.1.call-done, bf16[4096,256]{1,0:T(8,128)(2,1)} %dynamic-slice_bitcast_fusion, bf16[4096,384]{1,0:T(8,128)(2,1)} %bitcast.296), kind=kOutput, calls=%fused_computation.48 | convolution fusion | flops 10749214720 | bytes 24641536 | tf_op jit(solution)/shard_map/dot_general | solution.py:37
  123.1 1.5 slice_bitcast_fusion
  124.6 2.3 slice.65
  126.9 0.4 copy.21
  127.3 4.0 fusion.103
  131.4 1.9 copy.8
  133.3 2.6 copy.10
  135.9 4.7 fusion.9
  140.6 2.8 fusion.11
  143.4 9.8 %fusion.8 = (f32[3]{0:T(128)}, f32[3,512]{1,0:T(4,128)S(1)}, f32[3,512]{1,0:T(4,128)S(1)}, f32[3]{0:T(128)}) fusion(f32[2048,512,3]{1,0,2:T(8,128)S(1)} %get-tuple-element.19, pred[512,2048]{0,1:T(8,128)(4,1)S(1)} %copy-done.5, f32[3,512]{1,0:T(4,128)S(1)} %copy-done.11, f32[3,512]{1,0:T(4,128)S(1)} %get-tuple-element.22, ...), kind=kLoop, calls=%fused_computation.16 | loop fusion | flops 31454200 | bytes 27287576 | tf_op jit(solution)/shard_map/reduce_max | solution.py:82
  153.2 4.8 fusion.61
  158.0 4.4 convolution_convert_fusion.3
  162.4 0.0 reduce-scatter.5.cloned.1.call-update
  162.4 0.0 reduce-scatter.9.cloned.1.call-start
  162.5 0.1 iota_add_fusion.1
  162.5 0.1 add.157
  162.6 0.1 iota_add_fusion
  162.7 0.1 add.163
  162.8 1.8 iota_compare_fusion.1
  164.6 1.8 iota_compare_fusion
  166.4 2.3 copy.12
  168.7 2.5 copy.14
  171.2 4.8 fusion.13
  176.1 2.8 fusion.15
  178.9 9.1 %fusion.12 = (f32[3]{0:T(128)S(1)}, f32[3,512]{1,0:T(4,128)S(1)}, f32[3,512]{1,0:T(4,128)S(1)}, f32[3]{0:T(128)S(1)}) fusion(f32[2048,512,3]{1,0,2:T(8,128)S(1)} %get-tuple-element.21, pred[512,2048]{0,1:T(8,128)(4,1)S(1)} %copy-done.6, f32[3,512]{1,0:T(4,128)S(1)} %copy-done.12, f32[3,512]{1,0:T(4,128)S(1)} %get-tuple-element.24, ...), kind=kLoop, calls=%fused_computation.20 | loop fusion | flops 31454200 | bytes 27287576 | tf_op jit(solution)/shard_map/reduce_max | solution.py:82
  188.0 4.8 fusion.73
  192.8 4.3 convolution_convert_fusion.1
  197.1 0.0 reduce-scatter.9.cloned.1.call-update
  197.2 0.2 reduce-scatter.7.cloned.1.call-start
  197.4 8.6 %fusion.67 = bf16[512,1,3,128]{0,3,2,1:T(8,128)(2,1)S(1)} fusion(f32[2048,512,3]{1,0,2:T(8,128)} %copy-done.1, f32[3,512]{1,0:T(4,128)S(1)} %get-tuple-element.22, pred[512,2048]{0,1:T(8,128)(4,1)} %iota_compare_fusion.2, f32[512,3]{0,1:T(4,128)S(1)} %bitcast.292, bf16[2048,1,2,128]{0,3,2,1:T(8,128)(2,1)} %bitcast.279), kind=kOutput, calls=%fused_computation.68 | convolution fusion | flops 818282496 | bytes 14561280 | tf_op jit(solution)/shard_map/kgqs,skd->qkgd/dot_general | solution.py:74
  206.0 4.3 convolution_convert_fusion.2
  210.4 0.0 reduce-scatter.11.cloned.1.call-start
  210.4 8.7 %fusion.79 = bf16[512,1,3,128]{0,3,2,1:T(8,128)(2,1)S(1)} fusion(f32[2048,512,3]{1,0,2:T(8,128)} %copy-done.2, f32[3,512]{1,0:T(4,128)S(1)} %get-tuple-element.24, pred[512,2048]{0,1:T(8,128)(4,1)} %iota_compare_fusion, f32[512,3]{0,1:T(4,128)S(1)} %bitcast.293, bf16[2048,1,2,128]{0,3,2,1:T(8,128)(2,1)} %bitcast.280), kind=kOutput, calls=%fused_computation.72 | convolution fusion | flops 818282496 | bytes 14561280 | tf_op jit(solution)/shard_map/kgqs,skd->qkgd/dot_general | solution.py:74
  219.1 4.4 convolution_convert_fusion
  223.5 2.8 convert_element_type.72
  226.4 7.7 %reduce-scatter.5.cloned.1.call-done = bf16[32,4096]{1,0:T(8,128)(2,1)} async-done(((bf16[512,4096]{1,0:T(8,128)(2,1)}), bf16[32,4096]{1,0:T(8,128)(2,1)}) %reduce-scatter.5.cloned.1.call-update) | async-done | bytes 262160 | tf_op jit(solution)/shard_map/reduce_scatter | solution.py:84
  234.1 72.0 %reduce-scatter.9.cloned.1.call-done = bf16[32,4096]{1,0:T(8,128)(2,1)} async-done(((bf16[512,4096]{1,0:T(8,128)(2,1)}), bf16[32,4096]{1,0:T(8,128)(2,1)}) %reduce-scatter.9.cloned.1.call-update) | async-done | bytes 262160 | tf_op jit(solution)/shard_map/reduce_scatter | solution.py:84
  306.0 71.7 %reduce-scatter.7.cloned.1.call-done = bf16[32,4096]{1,0:T(8,128)(2,1)} async-done(((bf16[512,4096]{1,0:T(8,128)(2,1)}), bf16[32,4096]{1,0:T(8,128)(2,1)}) %reduce-scatter.7.cloned.1.call-update) | async-done | bytes 262160 | tf_op jit(solution)/shard_map/reduce_scatter | solution.py:84
  377.8 71.8 %reduce-scatter.11.cloned.1.call-done = bf16[32,4096]{1,0:T(8,128)(2,1)} async-done(((bf16[512,4096]{1,0:T(8,128)(2,1)}), bf16[32,4096]{1,0:T(8,128)(2,1)}) %reduce-scatter.11.cloned.1.call-update) | async-done | bytes 262160 | tf_op jit(solution)/shard_map/reduce_scatter | solution.py:84
  449.6 2.0 fusion.89
  451.6 1.5 collective-permute-start.3
  453.1 1.6 collective-permute-start.2
  454.8 1.4 collective-permute-start.1
  456.1 0.2 collective-permute-start
  456.3 3.0 collective-permute-start.4
  459.3 2.2 collective-permute-done.4
  461.5 0.5 max.3
  462.0 0.1 collective-permute-done.3
  462.0 5.6 %collective-permute-done.2 = bf16[32,4096]{1,0:T(8,128)(2,1)S(1)} collective-permute-done((bf16[32,4096]{1,0:T(8,128)(2,1)S(1)}, bf16[32,4096]{1,0:T(8,128)(2,1)S(1)}, u32[]{:S(2)}, u32[]{:S(2)}) %collective-permute-start.2) | collective-permute-done | bytes 262176 | tf_op jit(solution)/shard_map/ppermute | solution.py:16
  467.7 5.4 %collective-permute-done.1 = bf16[32,4096]{1,0:T(8,128)(2,1)S(1)} collective-permute-done((bf16[32,4096]{1,0:T(8,128)(2,1)S(1)}, bf16[32,4096]{1,0:T(8,128)(2,1)S(1)}, u32[]{:S(2)}, u32[]{:S(2)}) %collective-permute-start.1) | collective-permute-done | bytes 262176 | tf_op jit(solution)/shard_map/ppermute | solution.py:16
  473.0 2.8 collective-permute-done
  475.8 1.0 maximum_bitcast_fusion
  (39 shorter events, 0.1 us)
Async XLA Ops:
  7.2 150.8 %copy-start = (bf16[1,384,4096]{2,1,0:T(8,128)(2,1)S(1)}, bf16[1,384,4096]{2,1,0:T(8,128)(2,1)}, u32[]{:S(2)}) copy-start(bf16[1,384,4096]{2,1,0:T(8,128)(2,1)} %param.9) | copy-start | bytes 9437188
  7.2 98.5 %all-gather.2.cloned.1.call-start = ((), (), s32[]{:S(2)}) async-start(), calls=%async_computation.4 | async-start | bytes 17825792 | tf_op jit(solution)/shard_map/all_gather | solution.py:38
  11.5 222.6 %reduce-scatter.5.cloned.1.call-start = ((), (), s32[]{:S(2)}) async-start(), calls=%async_computation.5 | async-start | bytes 4456448 | tf_op jit(solution)/shard_map/reduce_scatter | solution.py:84
  135.9 4.7 copy-start.3
  135.9 4.7 copy-start.7
  135.9 4.7 copy-start.9
  140.6 2.9 copy-start.5
  140.6 2.9 copy-start.11
  143.4 9.8 %copy-start.1 = (f32[2048,512,3]{1,0,2:T(8,128)}, f32[2048,512,3]{1,0,2:T(8,128)S(1)}, u32[]{:S(2)}) copy-start(f32[2048,512,3]{1,0,2:T(8,128)S(1)} %get-tuple-element.23) | copy-start | bytes 37748740
  162.4 143.6 %reduce-scatter.9.cloned.1.call-start = ((), (), s32[]{:S(2)}) async-start(), calls=%async_computation.7 | async-start | bytes 4456448 | tf_op jit(solution)/shard_map/reduce_scatter | solution.py:84
  171.2 4.8 copy-start.4
  171.2 4.8 copy-start.8
  171.2 4.8 copy-start.10
  176.0 2.9 copy-start.6
  176.0 2.9 copy-start.12
  178.9 9.1 %copy-start.2 = (f32[2048,512,3]{1,0,2:T(8,128)}, f32[2048,512,3]{1,0,2:T(8,128)S(1)}, u32[]{:S(2)}) copy-start(f32[2048,512,3]{1,0,2:T(8,128)S(1)} %get-tuple-element.25) | copy-start | bytes 37748740
  197.2 180.6 %reduce-scatter.7.cloned.1.call-start = ((), (), s32[]{:S(2)}) async-start(), calls=%async_computation.6 | async-start | bytes 4456448 | tf_op jit(solution)/shard_map/reduce_scatter | solution.py:84
  210.4 239.2 %reduce-scatter.11.cloned.1.call-start = ((), (), s32[]{:S(2)}) async-start(), calls=%async_computation.8 | async-start | bytes 4456448 | tf_op jit(solution)/shard_map/reduce_scatter | solution.py:84
  219.1 237.2 %copy-start.13 = (f32[3]{0:T(128)S(1)}, f32[3]{0:T(128)}, u32[]{:S(2)}) copy-start(f32[3]{0:T(128)} %get-tuple-element.4) | copy-start | bytes 40
  219.1 237.2 %copy-start.14 = (f32[3]{0:T(128)S(1)}, f32[3]{0:T(128)}, u32[]{:S(2)}) copy-start(f32[3]{0:T(128)} %get-tuple-element.27) | copy-start | bytes 40
  451.6 10.5 %collective-permute-start.3 = (bf16[32,4096]{1,0:T(8,128)(2,1)S(1)}, bf16[32,4096]{1,0:T(8,128)(2,1)S(1)}, u32[]{:S(2)}, u32[]{:S(2)}) collective-permute-start(bf16[32,4096]{1,0:T(8,128)(2,1)S(1)} %get-tuple-element.13), channel_id=1, source_target_pairs={{48,0},{0,16},{16,32},{32,48},{49,1},{1,17},{17,33},{33,49},{50,2}... | collective-permute-start | bytes 786440 | tf_op jit(solution)/shard_map/ppermute | solution.py:16
  453.1 14.5 %collective-permute-start.2 = (bf16[32,4096]{1,0:T(8,128)(2,1)S(1)}, bf16[32,4096]{1,0:T(8,128)(2,1)S(1)}, u32[]{:S(2)}, u32[]{:S(2)}) collective-permute-start(bf16[32,4096]{1,0:T(8,128)(2,1)S(1)} %get-tuple-element.11), channel_id=1, source_target_pairs={{48,0},{0,16},{16,32},{32,48},{49,1},{1,17},{17,33},{33,49},{50,2}... | collective-permute-start | bytes 786440 | tf_op jit(solution)/shard_map/ppermute | solution.py:16
  454.8 18.3 %collective-permute-start.1 = (bf16[32,4096]{1,0:T(8,128)(2,1)S(1)}, bf16[32,4096]{1,0:T(8,128)(2,1)S(1)}, u32[]{:S(2)}, u32[]{:S(2)}) collective-permute-start(bf16[32,4096]{1,0:T(8,128)(2,1)S(1)} %get-tuple-element.12), channel_id=1, source_target_pairs={{48,0},{0,16},{16,32},{32,48},{49,1},{1,17},{17,33},{33,49},{50,2}... | collective-permute-start | bytes 786440 | tf_op jit(solution)/shard_map/ppermute | solution.py:16
  456.1 19.7 %collective-permute-start = (bf16[32,4096]{1,0:T(8,128)(2,1)S(1)}, bf16[32,4096]{1,0:T(8,128)(2,1)S(1)}, u32[]{:S(2)}, u32[]{:S(2)}) collective-permute-start(bf16[32,4096]{1,0:T(8,128)(2,1)S(1)} %get-tuple-element.10), channel_id=1, source_target_pairs={{48,0},{0,16},{16,32},{32,48},{49,1},{1,17},{17,33},{33,49},{50,2}... | collective-permute-start | bytes 786440 | tf_op jit(solution)/shard_map/ppermute | solution.py:16
  456.3 5.2 %collective-permute-start.4 = (f32[1,3]{1,0:T(1,128)S(1)}, f32[1,3]{1,0:T(1,128)S(1)}, u32[]{:S(2)}, u32[]{:S(2)}) collective-permute-start(f32[1,3]{1,0:T(1,128)S(1)} %maximum_bitcast_fusion.1), channel_id=1, source_target_pairs={{64,0},{0,64},{65,1},{1,65},{66,2},{2,66},{67,3},{3,67},{68,4},{4,... | collective-permute-start | bytes 44 | tf_op jit(solution)/shard_map/ppermute | solution.py:16
Sparse Core Ops, SparseCore 0:
  11.6 94.0 all-gather.1
  162.5 71.5 reduce-scatter.4
  236.5 69.5 reduce-scatter.8
  308.3 69.4 reduce-scatter.6
  380.0 69.4 reduce-scatter.10

commit v2 on v0

--- a/solution.py
+++ b/solution.py
@@ -3,16 +3,33 @@
 import jax
 import jax.numpy as jnp
 from jax import lax
+from jax.sharding import Mesh
 from jax.sharding import PartitionSpec as P
 
 HD = 128
 GROUP = 6
+CHIPS = ("ty", "tx")
+CORE = "tc"
+TENSOR = CHIPS + (CORE,)
 
 
 def from_behind(block, axis, distance):
     devices = range(lax.axis_size(axis))
     route = [((i - distance) % len(devices), i) for i in devices]
     return lax.ppermute(block, axis, route)
+
+
+def scatter_sum(partial):
+    n_chips = lax.axis_size(CHIPS)
+    rows = partial.shape[0] // (2 * n_chips)
+    core = lax.axis_index(CORE)
+    halves = partial.reshape(n_chips, 2, rows, partial.shape[1])
+    keep = lax.dynamic_index_in_dim(halves, core, 1, keepdims=False)
+    give = lax.dynamic_index_in_dim(halves, 1 - core, 1, keepdims=False)
+    got = lax.ppermute(give, CORE, [(0, 1), (1, 0)])
+    pair = (keep.astype(jnp.float32) + got.astype(jnp.float32)).astype(jnp.bfloat16)
+    swapped = lax.all_to_all(pair, CHIPS, 0, 0, tiled=True)
+    return jnp.sum(swapped.astype(jnp.float32), 0)
 
 
 def on_device(tokens, norm_gain, query_weight, kv_weight, out_weight):
@@ -28,12 +45,12 @@
     kv_dev = max(1, heads_dev // GROUP)
     kv_cols = kv_dev * 2 * HD
     query_cols = heads_dev * HD
-    tensor_id = lax.axis_index("tensor")
+    tensor_id = lax.axis_index(TENSOR)
     kv_start = tensor_id * heads_dev // GROUP
     kv_local = lax.dynamic_slice_in_dim(kv_weight[0], kv_start * 2 * HD, kv_cols, 1)
     joined = jnp.concatenate([query_local, kv_local], 1)
     projected = jnp.dot(
-        lax.all_gather(normed, "tensor", axis=0, tiled=True),
+        lax.all_gather(normed, TENSOR, axis=0, tiled=True),
         joined,
         preferred_element_type=jnp.float32,
     ).astype(jnp.bfloat16)
@@ -74,31 +91,33 @@
     outputs, head_peaks = lax.map(attend, starts)
     attended = outputs.reshape(seq_len, query_cols)
     peaks_local = jnp.max(head_peaks, axis=0)
+    peak_all = jnp.maximum(peaks_local, from_behind(peaks_local, "dp", 1))
     out_local = out_weight[0]
-    summed = lax.psum_scatter(
-        jnp.dot(attended, out_local, preferred_element_type=jnp.float32).astype(jnp.bfloat16),
-        "tensor",
-        scatter_dimension=0,
-        tiled=True,
-    ).astype(jnp.float32)
+    summed = scatter_sum(
+        jnp.dot(attended, out_local, preferred_element_type=jnp.float32).astype(jnp.bfloat16)
+    )
     result = (wide_in + summed).astype(jnp.bfloat16)
-    peak_all = lax.pmax(peaks_local, "dp")
     passed = from_behind(result, "pipe", 1)
     return (passed[None, None], peak_all)
 
 
 def solution(mesh):
+    n_tensor = mesh.shape["tensor"]
+    fine = Mesh(
+        mesh.devices.reshape(mesh.shape["dp"], mesh.shape["pipe"], n_tensor // 4, 2, 2),
+        ("dp", "pipe") + TENSOR,
+    )
     placed = (
-        P("dp", "pipe", "tensor", None),
+        P("dp", "pipe", TENSOR, None),
         P("pipe", None),
-        P("pipe", None, "tensor"),
+        P("pipe", None, TENSOR),
         P("pipe", None, None),
-        P("pipe", "tensor", None),
+        P("pipe", TENSOR, None),
     )
     return jax.shard_map(
         on_device,
-        mesh=mesh,
+        mesh=fine,
         in_specs=placed,
-        out_specs=(P("dp", "pipe", "tensor", None), P("pipe", "tensor")),
+        out_specs=(P("dp", "pipe", TENSOR, None), P("pipe", TENSOR)),
         check_vma=False,
     )

time: 437 us -> 383 us (0.88)
  waiting for transfers between devices: 291 us -> 125 us
  blocking collectives: 6.93 us -> 99.3 us
  local copies, waits for them, and re-layouts: 21.4 us -> 30.3 us
  other arithmetic: 28.6 us -> 36.4 us
    reduce_scatter x1 -> x0, waiting for transfers between devices: 183 us -> none  [on_device(): lax.psum_scatter(jnp.dot(attended, out_local, preferred_element_type=jnp....]
    all_to_all x0 -> x1, blocking collectives: none -> 99.3 us  [scatter_sum(): swapped = lax.all_to_all(pair, CHIPS, 0, 0, tiled=True)]
    ppermute x0 -> x1, waiting for transfers between devices: none -> 13.3 us  [scatter_sum(): got = lax.ppermute(give, CORE, [(0, 1), (1, 0)])]
    squeeze x0 -> x1, local copies, waits for them, and re-layouts: none -> 7.7 us  [scatter_sum(): give = lax.dynamic_index_in_dim(halves, 1 - core, 1, keepdims=False)]
    convert_element_type x0 -> x1, other arithmetic: none -> 7.5 us  [scatter_sum(): (keep.astype(jnp.float32) + got.astype(jnp.float32)).astype(jnp.bfloat16)]
    pmax x1 -> x0, blocking collectives: 6.93 us -> none  [on_device(): peak_all = lax.pmax(peaks_local, 'dp')]
    ppermute x1 -> x2, waiting for transfers between devices: 16.3 us -> 20.6 us  [from_behind(): return lax.ppermute(block, axis, route)]
  transfers between devices with their start and end apart: 3 -> 4, of which waited for: 3 -> 4; matrix products, arithmetic and copies ran while one was open for 1% -> 1% of each run, Pallas kernels for 0% -> 0%
where the time goes in v2:
time: 383 us; the launch traced here: 382 us
  waiting for transfers between devices  125 us (33%)
  blocking collectives  99.3 us (26%)
  matrix products  65.2 us (17%)
  other arithmetic  36.4 us (10%)
  local copies, waits for them, and re-layouts  30.3 us (8%)
  between operations  14.2 us (4%)
  loops' own time  7.59 us (2%)
  starting transfers between devices  4.59 us (1%)
    all_to_all x1, blocking collectives, scatter_sum(): swapped = lax.all_to_all(pair, CHIPS, 0, 0, tiled=True)  99.3 us
    all_gather x1, waiting for transfers between devices, on_device(): lax.all_gather(normed, TENSOR, axis=0, tiled=True)  91.1 us
    ppermute x2, waiting for transfers between devices, from_behind(): return lax.ppermute(block, axis, route)  20.6 us
    dot_general x4, matrix products, attend(): jnp.einsum('qkgd,skd->kgqs', query_block, key_heads, preferred_element_ty...  18.6 us
    dot_general x1, matrix products, on_device(): jnp.dot(lax.all_gather(normed, TENSOR, axis=0, tiled=True), joined, prefe...  17.3 us
    dot_general x4, matrix products, attend(): jnp.einsum('kgqs,skd->qkgd', expw.astype(jnp.bfloat16), value_heads, pref...  16.9 us
    reduce_max x4, other arithmetic, attend(): return (blended.astype(jnp.bfloat16), jnp.max(row_max[..., 0], axis=2))  16.4 us
    ppermute x1, waiting for transfers between devices, scatter_sum(): got = lax.ppermute(give, CORE, [(0, 1), (1, 0)])  13.3 us
  transfers between devices with their start and end apart: 4, of which 4 were waited for; matrix products, arithmetic and copies ran while one was open for 1% of the time, Pallas kernels for 0%

profile of v2, /device:TPU:0, one launch (start us, length us, event | category | flops | bytes accessed | tf_op | source)
XLA Modules:
  0.0 382.5 jit_solution(17441253408109861480)
XLA Ops:
  7.2 0.0 copy-start
  7.2 0.0 all-gather.2.cloned.1.call-start
  7.2 1.7 fusion.40
  8.9 2.5 fusion.42
  11.4 0.0 all-gather.2.cloned.1.call-update
  11.5 3.0 dynamic-slice_bitcast_fusion.1
  14.6 91.1 %all-gather.2.cloned.1.call-done = bf16[2048,4096]{1,0:T(8,128)(2,1)} async-done(((bf16[128,4096]{1,0:T(8,128)(2,1)}), bf16[2048,4096]{1,0:T(8,128)(2,1)}) %all-gather.2.cloned.1.call-update) | async-done | bytes 16777232 | tf_op jit(solution)/shard_map/all_gather | solution.py:53
  105.6 17.3 %fusion.36 = bf16[2048,640]{0,1:T(8,128)(2,1)} fusion(bf16[2048,4096]{1,0:T(8,128)(2,1)} %all-gather.2.cloned.1.call-done, bf16[4096,256]{1,0:T(8,128)(2,1)} %dynamic-slice_bitcast_fusion.1, bf16[4096,384]{1,0:T(8,128)(2,1)} %bitcast.149), kind=kOutput, calls=%fused_computation.34 | convolution fusion | flops 10749214720 | bytes 24641536 | tf_op jit(solution)/shard_map/dot_general | solution.py:52
  122.9 1.3 slice.17
  124.2 2.7 slice.16
  126.9 1.0 fusion.45
  128.0 2.1 copy.16
  130.0 2.0 copy.15
  132.1 67.1 %while.12 = (s32[]{:T(128)}, bf16[4,512,1,3,128]{4,1,3,2,0:T(8,128)(2,1)}, f32[4,1,3]{2,1,0:T(1,128)S(1)}, s32[4]{0:T(128)S(1)}, bf16[2048,1,3,128]{0,3,2,1:T(8,...) while((s32[]{:T(128)}, ...), condition=%wide.region_5.6_spmd, body=%wide.region_1.5_spmd.sunk | while | flops 1649800704 | bytes 45911252 | solution.py:91
  132.1 0.6 dynamic_slice.35
  134.5 0.6 iota_add_fusion.2
  135.1 0.7 iota_compare_fusion.2
  135.8 4.7 %fusion.55 = (f32[3,512]{1,0:T(4,128)S(1)}, f32[512,3,2048]{2,0,1:T(8,128)S(1)}) fusion(pred[512,2048]{1,0:T(8,128)(4,1)S(1)} %iota_compare_fusion.2, bf16[2048,1,128]{2,0,1:T(8,128)(2,1)} %get-tuple-element.152, bf16[2048,1,3,128]{0,3,2,1:T(8,128)(2,1)} %get-tuple-element.151, s32[]{:T(128)S(6)} %select_n.55), kind=kOutput, calls=%fused_computation.5.clone.1 | convolution fusion | flops 814742016 | bytes 14555140 | tf_op jit(solution)/shard_map/while/body/eval_jaxpr/qkgd,skd->kgqs/dot_general | solution.py:71
  140.5 0.0 copy-start.2
  140.5 4.1 %fusion.56 = (f32[3]{0:T(128)S(1)}, f32[3,512]{1,0:T(4,128)S(1)}) fusion(f32[512,3,2048]{2,0,1:T(8,128)S(1)} %get-tuple-element.123, pred[512,2048]{1,0:T(8,128)(4,1)S(1)} %iota_compare_fusion.2, f32[3,512]{1,0:T(4,128)S(1)} %get-tuple-element.124), kind=kLoop, calls=%fused_computation.4.clone.1 | loop fusion | flops 15727101 | bytes 13643788 | tf_op jit(solution)/shard_map/while/body/eval_jaxpr/reduce_max | solution.py:88
  144.6 0.0 copy-done.2
  144.6 4.2 %fusion.57 = bf16[4,512,1,3,128]{4,1,3,2,0:T(8,128)(2,1)} fusion(bf16[4,512,1,3,128]{4,1,3,2,0:T(8,128)(2,1)} %get-tuple-element.138, s32[]{:T(128)S(6)} %copy.23, f32[512,3,2048]{2,0,1:T(8,128)S(1)} %get-tuple-element.123, f32[3,512]{1,0:T(4,128)S(1)} %get-tuple-element.124, pred[512,2048]{1,0:T(8,128)(4,1)S(1)} %iota_compare_fusion.2, ...), kind=kOutput, calls=%fused_computation.14.clone.1 | convolution fusion | flops 818282496 | bytes 14561284 | tf_op jit(solution)/shard_map/while/body/eval_jaxpr/kgqs,skd->qkgd/dot_general | solution.py:81
  148.8 0.6 dynamic_slice.35
  151.3 0.6 iota_add_fusion.2
  151.9 0.7 iota_compare_fusion.2
  152.6 4.7 %fusion.55 = (f32[3,512]{1,0:T(4,128)S(1)}, f32[512,3,2048]{2,0,1:T(8,128)S(1)}) fusion(pred[512,2048]{1,0:T(8,128)(4,1)S(1)} %iota_compare_fusion.2, bf16[2048,1,128]{2,0,1:T(8,128)(2,1)} %get-tuple-element.152, bf16[2048,1,3,128]{0,3,2,1:T(8,128)(2,1)} %get-tuple-element.151, s32[]{:T(128)S(6)} %select_n.55), kind=kOutput, calls=%fused_computation.5.clone.1 | convolution fusion | flops 814742016 | bytes 14555140 | tf_op jit(solution)/shard_map/while/body/eval_jaxpr/qkgd,skd->kgqs/dot_general | solution.py:71
  157.3 0.0 copy-start.2
  157.3 4.1 %fusion.56 = (f32[3]{0:T(128)S(1)}, f32[3,512]{1,0:T(4,128)S(1)}) fusion(f32[512,3,2048]{2,0,1:T(8,128)S(1)} %get-tuple-element.123, pred[512,2048]{1,0:T(8,128)(4,1)S(1)} %iota_compare_fusion.2, f32[3,512]{1,0:T(4,128)S(1)} %get-tuple-element.124), kind=kLoop, calls=%fused_computation.4.clone.1 | loop fusion | flops 15727101 | bytes 13643788 | tf_op jit(solution)/shard_map/while/body/eval_jaxpr/reduce_max | solution.py:88
  161.4 0.0 copy-done.2
  161.4 4.2 %fusion.57 = bf16[4,512,1,3,128]{4,1,3,2,0:T(8,128)(2,1)} fusion(bf16[4,512,1,3,128]{4,1,3,2,0:T(8,128)(2,1)} %get-tuple-element.138, s32[]{:T(128)S(6)} %copy.23, f32[512,3,2048]{2,0,1:T(8,128)S(1)} %get-tuple-element.123, f32[3,512]{1,0:T(4,128)S(1)} %get-tuple-element.124, pred[512,2048]{1,0:T(8,128)(4,1)S(1)} %iota_compare_fusion.2, ...), kind=kOutput, calls=%fused_computation.14.clone.1 | convolution fusion | flops 818282496 | bytes 14561284 | tf_op jit(solution)/shard_map/while/body/eval_jaxpr/kgqs,skd->qkgd/dot_general | solution.py:81
  165.6 0.6 dynamic_slice.35
  168.1 0.6 iota_add_fusion.2
  168.7 0.7 iota_compare_fusion.2
  169.3 4.7 %fusion.55 = (f32[3,512]{1,0:T(4,128)S(1)}, f32[512,3,2048]{2,0,1:T(8,128)S(1)}) fusion(pred[512,2048]{1,0:T(8,128)(4,1)S(1)} %iota_compare_fusion.2, bf16[2048,1,128]{2,0,1:T(8,128)(2,1)} %get-tuple-element.152, bf16[2048,1,3,128]{0,3,2,1:T(8,128)(2,1)} %get-tuple-element.151, s32[]{:T(128)S(6)} %select_n.55), kind=kOutput, calls=%fused_computation.5.clone.1 | convolution fusion | flops 814742016 | bytes 14555140 | tf_op jit(solution)/shard_map/while/body/eval_jaxpr/qkgd,skd->kgqs/dot_general | solution.py:71
  174.0 0.0 copy-start.2
  174.0 4.1 %fusion.56 = (f32[3]{0:T(128)S(1)}, f32[3,512]{1,0:T(4,128)S(1)}) fusion(f32[512,3,2048]{2,0,1:T(8,128)S(1)} %get-tuple-element.123, pred[512,2048]{1,0:T(8,128)(4,1)S(1)} %iota_compare_fusion.2, f32[3,512]{1,0:T(4,128)S(1)} %get-tuple-element.124), kind=kLoop, calls=%fused_computation.4.clone.1 | loop fusion | flops 15727101 | bytes 13643788 | tf_op jit(solution)/shard_map/while/body/eval_jaxpr/reduce_max | solution.py:88
  178.1 0.0 copy-done.2
  178.2 4.2 %fusion.57 = bf16[4,512,1,3,128]{4,1,3,2,0:T(8,128)(2,1)} fusion(bf16[4,512,1,3,128]{4,1,3,2,0:T(8,128)(2,1)} %get-tuple-element.138, s32[]{:T(128)S(6)} %copy.23, f32[512,3,2048]{2,0,1:T(8,128)S(1)} %get-tuple-element.123, f32[3,512]{1,0:T(4,128)S(1)} %get-tuple-element.124, pred[512,2048]{1,0:T(8,128)(4,1)S(1)} %iota_compare_fusion.2, ...), kind=kOutput, calls=%fused_computation.14.clone.1 | convolution fusion | flops 818282496 | bytes 14561284 | tf_op jit(solution)/shard_map/while/body/eval_jaxpr/kgqs,skd->qkgd/dot_general | solution.py:81
  182.4 0.6 dynamic_slice.35
  184.8 0.6 iota_add_fusion.2
  185.5 0.7 iota_compare_fusion.2
  186.1 4.6 %fusion.55 = (f32[3,512]{1,0:T(4,128)S(1)}, f32[512,3,2048]{2,0,1:T(8,128)S(1)}) fusion(pred[512,2048]{1,0:T(8,128)(4,1)S(1)} %iota_compare_fusion.2, bf16[2048,1,128]{2,0,1:T(8,128)(2,1)} %get-tuple-element.152, bf16[2048,1,3,128]{0,3,2,1:T(8,128)(2,1)} %get-tuple-element.151, s32[]{:T(128)S(6)} %select_n.55), kind=kOutput, calls=%fused_computation.5.clone.1 | convolution fusion | flops 814742016 | bytes 14555140 | tf_op jit(solution)/shard_map/while/body/eval_jaxpr/qkgd,skd->kgqs/dot_general | solution.py:71
  190.8 0.0 copy-start.2
  190.8 4.1 %fusion.56 = (f32[3]{0:T(128)S(1)}, f32[3,512]{1,0:T(4,128)S(1)}) fusion(f32[512,3,2048]{2,0,1:T(8,128)S(1)} %get-tuple-element.123, pred[512,2048]{1,0:T(8,128)(4,1)S(1)} %iota_compare_fusion.2, f32[3,512]{1,0:T(4,128)S(1)} %get-tuple-element.124), kind=kLoop, calls=%fused_computation.4.clone.1 | loop fusion | flops 15727101 | bytes 13643788 | tf_op jit(solution)/shard_map/while/body/eval_jaxpr/reduce_max | solution.py:88
  194.9 0.0 copy-done.2
  194.9 4.2 %fusion.57 = bf16[4,512,1,3,128]{4,1,3,2,0:T(8,128)(2,1)} fusion(bf16[4,512,1,3,128]{4,1,3,2,0:T(8,128)(2,1)} %get-tuple-element.138, s32[]{:T(128)S(6)} %copy.23, f32[512,3,2048]{2,0,1:T(8,128)S(1)} %get-tuple-element.123, f32[3,512]{1,0:T(4,128)S(1)} %get-tuple-element.124, pred[512,2048]{1,0:T(8,128)(4,1)S(1)} %iota_compare_fusion.2, ...), kind=kOutput, calls=%fused_computation.14.clone.1 | convolution fusion | flops 818282496 | bytes 14561284 | tf_op jit(solution)/shard_map/while/body/eval_jaxpr/kgqs,skd->qkgd/dot_general | solution.py:81
  199.1 3.9 %copy.13 = bf16[4,512,1,3,128]{1,0,4,3,2:T(4,128)(2,1)} copy(bf16[4,512,1,3,128]{4,1,3,2,0:T(8,128)(2,1)} %get-tuple-element.40) | data formatting | bytes 3145728 | tf_op jit(solution)/shard_map/while | solution.py:91
  203.0 1.8 copy.17
  204.9 0.0 copy-done
  204.9 12.4 %convolution_convert_fusion = bf16[2048,4096]{1,0:T(8,128)(2,1)} fusion(bf16[2048,384]{0,1:T(8,128)(2,1)S(1)} %bitcast.143, bf16[1,384,4096]{2,1,0:T(8,128)(2,1)S(1)} %copy-done), kind=kOutput, calls=%fused_computation.28 | convolution fusion | flops 6450839552 | bytes 21495808 | tf_op jit(solution)/shard_map/dot_general | solution.py:97
  217.3 7.7 %dynamic-slice_bitcast_fusion = bf16[8,128,4096]{2,1,0:T(8,128)(2,1)} fusion(bf16[8,2,128,4096]{3,2,1,0:T(8,128)(2,1)} %bitcast.138, s32[]{:T(128)S(6)} %select_n.25), kind=kLoop, calls=%fused_computation.29 | loop fusion | bytes 16777220 | tf_op jit(solution)/shard_map/jit(dynamic_index_in_dim)/squeeze | solution.py:28
  225.0 0.2 collective-permute-start
  225.2 13.3 %collective-permute-done = bf16[8,128,4096]{2,1,0:T(8,128)(2,1)} collective-permute-done((bf16[8,128,4096]{2,1,0:T(8,128)(2,1)}, bf16[8,128,4096]{2,1,0:T(8,128)(2,1)}, u32[]{:S(2)}, u32[]{:S(2)}) %collective-permute-start) | collective-permute-done | bytes 8388640 | tf_op jit(solution)/shard_map/ppermute | solution.py:29
  238.5 7.5 %fusion.31 = bf16[8,128,4096]{2,1,0:T(8,128)(2,1)S(1)} fusion(bf16[8,128,4096]{2,1,0:T(8,128)(2,1)} %collective-permute-done, bf16[8,2,128,4096]{3,2,1,0:T(8,128)(2,1)} %bitcast.139, s32[]{:T(128)S(6)} %select_n.24), kind=kLoop, calls=%fused_computation.26 | loop fusion | flops 16777216 | bytes 25165828 | tf_op jit(solution)/shard_map/convert_element_type | solution.py:30
  246.0 99.3 %all_to_all.5 = bf16[8,128,4096]{2,1,0:T(8,128)(2,1)S(1)} all-to-all(bf16[8,128,4096]{2,1,0:T(8,128)(2,1)S(1)} %fusion.31), channel_id=1, replica_groups=mesh['dp'=2,'pipe'=4,'ty'=4,'tx'=2,'tc'=2] {'ty','tx'}, dimensions={0} | all-to-all | bytes 16777216 | tf_op jit(solution)/shard_map/all_to_all | solution.py:31
  345.3 1.5 convert_reduce_fusion
  346.7 0.0 copy-done.1
  346.7 1.2 fusion.43
  347.9 1.6 collective-permute-start.1
  349.5 2.7 collective-permute-start.2
  352.3 2.4 collective-permute-done.2
  354.6 0.5 bitcast_maximum_fusion
  355.2 18.2 %collective-permute-done.1 = bf16[128,4096]{1,0:T(8,128)(2,1)} collective-permute-done((bf16[128,4096]{1,0:T(8,128)(2,1)}, bf16[128,4096]{1,0:T(8,128)(2,1)}, u32[]{:S(2)}, u32[]{:S(2)}) %collective-permute-start.1) | collective-permute-done | bytes 1048608 | tf_op jit(solution)/shard_map/ppermute | solution.py:19
  373.3 2.3 copy.30
  (10 shorter events, 0.1 us)
Async XLA Ops:
  7.2 197.7 %copy-start = (bf16[1,384,4096]{2,1,0:T(8,128)(2,1)S(1)}, bf16[1,384,4096]{2,1,0:T(8,128)(2,1)}, u32[]{:S(2)}) copy-start(bf16[1,384,4096]{2,1,0:T(8,128)(2,1)} %param.11) | copy-start | bytes 9437188
  7.2 98.5 %all-gather.2.cloned.1.call-start = ((), (), s32[]{:S(2)}) async-start(), calls=%async_computation.1 | async-start | bytes 17825792 | tf_op jit(solution)/shard_map/all_gather | solution.py:53
  140.5 4.1 %copy-start.2 = (bf16[2048,1,128]{2,0,1:T(8,128)(2,1)S(1)}, bf16[2048,1,128]{2,0,1:T(8,128)(2,1)}, u32[]{:S(2)}) copy-start(bf16[2048,1,128]{2,0,1:T(8,128)(2,1)} %get-tuple-element.153) | copy-start | bytes 1572868 | tf_op jit(solution)/shard_map/while
  157.3 4.1 %copy-start.2 = (bf16[2048,1,128]{2,0,1:T(8,128)(2,1)S(1)}, bf16[2048,1,128]{2,0,1:T(8,128)(2,1)}, u32[]{:S(2)}) copy-start(bf16[2048,1,128]{2,0,1:T(8,128)(2,1)} %get-tuple-element.153) | copy-start | bytes 1572868 | tf_op jit(solution)/shard_map/while
  174.0 4.1 %copy-start.2 = (bf16[2048,1,128]{2,0,1:T(8,128)(2,1)S(1)}, bf16[2048,1,128]{2,0,1:T(8,128)(2,1)}, u32[]{:S(2)}) copy-start(bf16[2048,1,128]{2,0,1:T(8,128)(2,1)} %get-tuple-element.153) | copy-start | bytes 1572868 | tf_op jit(solution)/shard_map/while
  190.8 4.1 %copy-start.2 = (bf16[2048,1,128]{2,0,1:T(8,128)(2,1)S(1)}, bf16[2048,1,128]{2,0,1:T(8,128)(2,1)}, u32[]{:S(2)}) copy-start(bf16[2048,1,128]{2,0,1:T(8,128)(2,1)} %get-tuple-element.153) | copy-start | bytes 1572868 | tf_op jit(solution)/shard_map/while
  225.0 13.5 %collective-permute-start = (bf16[8,128,4096]{2,1,0:T(8,128)(2,1)}, bf16[8,128,4096]{2,1,0:T(8,128)(2,1)}, u32[]{:S(2)}, u32[]{:S(2)}) collective-permute-start(bf16[8,128,4096]{2,1,0:T(8,128)(2,1)} %dynamic-slice_bitcast_fusion), channel_id=1, source_target_pairs={{0,1},{1,0},{2,3},{3,2},{4,5},{5,4},{6,7},{7,6},{8,9},{9,8},{10,11... | collective-permute-start | bytes 25165832 | tf_op jit(solution)/shard_map/ppermute | solution.py:29
  345.3 1.5 copy-start.1
  347.9 25.4 %collective-permute-start.1 = (bf16[128,4096]{1,0:T(8,128)(2,1)}, bf16[128,4096]{1,0:T(8,128)(2,1)}, u32[]{:S(2)}, u32[]{:S(2)}) collective-permute-start(bf16[128,4096]{1,0:T(8,128)(2,1)} %fusion.43), channel_id=1, source_target_pairs={{48,0},{0,16},{16,32},{32,48},{49,1},{1,17},{17,33},{33,49},{50,2}... | collective-permute-start | bytes 3145736 | tf_op jit(solution)/shard_map/ppermute | solution.py:19
  349.5 5.1 %collective-permute-start.2 = (f32[1,3]{1,0:T(1,128)S(1)}, f32[1,3]{1,0:T(1,128)S(1)}, u32[]{:S(2)}, u32[]{:S(2)}) collective-permute-start(f32[1,3]{1,0:T(1,128)S(1)} %bitcast.148), channel_id=1, source_target_pairs={{64,0},{0,64},{65,1},{1,65},{66,2},{2,66},{67,3},{3,67},{68,4},{4,... | collective-permute-start | bytes 44 | tf_op jit(solution)/shard_map/ppermute | solution.py:19
Sparse Core Ops, SparseCore 0:
  11.6 94.0 all-gather.1

commit v3 on v2

--- a/solution.py
+++ b/solution.py
@@ -6,11 +6,13 @@
 from jax.sharding import Mesh
 from jax.sharding import PartitionSpec as P
 
+
 HD = 128
 GROUP = 6
 CHIPS = ("ty", "tx")
 CORE = "tc"
 TENSOR = CHIPS + (CORE,)
+N_BLOCKS = 2
 
 
 def from_behind(block, axis, distance):
@@ -28,11 +30,17 @@
     give = lax.dynamic_index_in_dim(halves, 1 - core, 1, keepdims=False)
     got = lax.ppermute(give, CORE, [(0, 1), (1, 0)])
     pair = (keep.astype(jnp.float32) + got.astype(jnp.float32)).astype(jnp.bfloat16)
-    swapped = lax.all_to_all(pair, CHIPS, 0, 0, tiled=True)
-    return jnp.sum(swapped.astype(jnp.float32), 0)
+    chip = lax.axis_index(CHIPS)
+    total = lax.dynamic_index_in_dim(pair, chip, 0, keepdims=False).astype(jnp.float32)
+    for k in range(1, n_chips):
+        send = lax.dynamic_index_in_dim(pair, (chip + k) % n_chips, 0, keepdims=False)
+        route = [(i, (i + k) % n_chips) for i in range(n_chips)]
+        got = lax.ppermute(send, CHIPS, route)
+        total = total + got.astype(jnp.float32)
+    return total
 
 
-def on_device(tokens, norm_gain, query_weight, kv_weight, out_weight):
+def on_device_body(tokens, norm_gain, query_weight, kv_weight, out_weight):
     inputs = tokens[0, 0]
     wide_in = inputs.astype(jnp.float32)
     normed = (
@@ -62,17 +70,26 @@
     kv_heads = keyvals.reshape(seq_len, kv_dev, 2, HD)
     key_heads = kv_heads[:, :, 0]
     value_heads = kv_heads[:, :, 1]
-    block_rows = min(512, seq_len)
     score_scale = 1.0 / math.sqrt(HD)
-
-    def attend(row_start):
-        query_block = lax.dynamic_slice_in_dim(query_heads, row_start, block_rows, 0)
+    out_local = out_weight[0]
+    n_dev = lax.axis_size(TENSOR)
+    local_rows = inputs.shape[0]
+    sub = local_rows // N_BLOCKS
+    block_rows = n_dev * sub
+    col_ids = jnp.arange(seq_len)
+    pieces = []
+    peaks = []
+    for b in range(N_BLOCKS):
+        query_block = query_heads.reshape(n_dev, local_rows, kv_dev, group_loc, HD)[
+            :, b * sub : (b + 1) * sub
+        ].reshape(block_rows, kv_dev, group_loc, HD)
+        row_ids = (
+            jnp.arange(n_dev)[:, None] * local_rows + b * sub + jnp.arange(sub)[None, :]
+        ).reshape(block_rows)
         scores = (
             jnp.einsum("qkgd,skd->kgqs", query_block, key_heads, preferred_element_type=jnp.float32)
             * score_scale
         )
-        row_ids = row_start + jnp.arange(block_rows)
-        col_ids = jnp.arange(seq_len)
         allowed = col_ids[None, :] <= row_ids[:, None]
         scores = jnp.where(allowed, scores, -jnp.inf)
         row_max = jnp.max(scores, axis=3, keepdims=True)
@@ -85,19 +102,15 @@
             preferred_element_type=jnp.float32,
         )
         blended = blended / jnp.transpose(row_sum, (2, 0, 1, 3))
-        return (blended.astype(jnp.bfloat16), jnp.max(row_max[..., 0], axis=2))
-
-    starts = jnp.arange(seq_len // block_rows) * block_rows
-    outputs, head_peaks = lax.map(attend, starts)
-    attended = outputs.reshape(seq_len, query_cols)
-    peaks_local = jnp.max(head_peaks, axis=0)
+        attended = blended.astype(jnp.bfloat16).reshape(block_rows, query_cols)
+        peaks.append(jnp.max(row_max[..., 0], axis=2))
+        partial = jnp.dot(attended, out_local, preferred_element_type=jnp.float32).astype(jnp.bfloat16)
+        summed = scatter_sum(partial)
+        result = (wide_in[b * sub : (b + 1) * sub] + summed).astype(jnp.bfloat16)
+        pieces.append(from_behind(result, "pipe", 1))
+    peaks_local = jnp.max(jnp.stack(peaks), axis=0)
     peak_all = jnp.maximum(peaks_local, from_behind(peaks_local, "dp", 1))
-    out_local = out_weight[0]
-    summed = scatter_sum(
-        jnp.dot(attended, out_local, preferred_element_type=jnp.float32).astype(jnp.bfloat16)
-    )
-    result = (wide_in + summed).astype(jnp.bfloat16)
-    passed = from_behind(result, "pipe", 1)
+    passed = jnp.concatenate(pieces, 0)
     return (passed[None, None], peak_all)
 
 
@@ -115,7 +128,7 @@
         P("pipe", TENSOR, None),
     )
     return jax.shard_map(
-        on_device,
+        on_device_body,
         mesh=fine,
         in_specs=placed,
         out_specs=(P("dp", "pipe", TENSOR, None), P("pipe", TENSOR)),

time: 383 us -> 390 us (1.018); the launches traced: 382 us -> 385 us
  blocking collectives: 99.3 us -> 0 us
  starting transfers between devices: 4.59 us -> 55.7 us
  waiting for transfers between devices: 125 us -> 156 us
  other arithmetic: 36.4 us -> 51.5 us
  matrix products: 65.2 us -> 75.5 us
  loops' own time: 7.59 us -> 0 us
    all_to_all x1 -> x0, blocking collectives: 99.3 us -> none  [scatter_sum(): swapped = lax.all_to_all(pair, CHIPS, 0, 0, tiled=True)]
    ppermute x0 -> x14, waiting for transfers between devices: none -> 50.7 us  [scatter_sum(): got = lax.ppermute(send, CHIPS, route)]
    ppermute x0 -> x14, starting transfers between devices: none -> 46.6 us  [scatter_sum(): got = lax.ppermute(send, CHIPS, route)]
    ppermute x1 -> x2, waiting for transfers between devices: 13.3 us -> 0.01 us  [scatter_sum(): got = lax.ppermute(give, CORE, [(0, 1), (1, 0)])]
    dot_general x10 -> x7, matrix products: 65.2 us -> 75.5 us  [the longest x2 24.4 us: on_device_body(): jnp.einsum('kgqs,skd->qkgd', expw.astype(jnp.bfloat16), value_heads, pref...]
    another operation x1 -> x0, loops' own time: 7.59 us -> none  [on_device(): outputs, head_peaks = lax.map(attend, starts)]
    convert_element_type x2 -> x3, other arithmetic: 3.71 us -> 10.7 us  [the longest x1 5.38 us: on_device_body(): result = (wide_in[b * sub:(b + 1) * sub] + summed).astype(jnp.bfloat16)]
    all_gather x1, waiting for transfers between devices: 91.1 us -> 84.5 us  [on_device_body(): lax.all_gather(normed, TENSOR, axis=0, tiled=True)]
  transfers between devices with their start and end apart: 4 -> 20, of which waited for: 4 -> 12; matrix products, arithmetic and copies ran while one was open for 1% -> 12% of each run, Pallas kernels for 0% -> 0%
where the time goes in v3:
time: 390 us; the launch traced here: 385 us
  waiting for transfers between devices  156 us (40%)
  matrix products  75.5 us (19%)
  starting transfers between devices  55.7 us (14%)
  other arithmetic  51.5 us (13%)
  local copies, waits for them, and re-layouts  31.6 us (8%)
  between operations  14.5 us (4%)
    all_gather x1, waiting for transfers between devices, on_device_body(): lax.all_gather(normed, TENSOR, axis=0, tiled=True)  84.5 us
    ppermute x14, waiting for transfers between devices, scatter_sum(): got = lax.ppermute(send, CHIPS, route)  50.7 us
    ppermute x14, starting transfers between devices, scatter_sum(): got = lax.ppermute(send, CHIPS, route)  46.6 us
    dot_general x2, matrix products, on_device_body(): jnp.einsum('kgqs,skd->qkgd', expw.astype(jnp.bfloat16), value_heads, pref...  24.4 us
    dot_general x2, matrix products, on_device_body(): jnp.einsum('qkgd,skd->kgqs', query_block, key_heads, preferred_element_ty...  23.6 us
    reduce_max x1, other arithmetic, on_device_body(): peaks.append(jnp.max(row_max[..., 0], axis=2))  22.2 us
    ppermute x3, waiting for transfers between devices, from_behind(): return lax.ppermute(block, axis, route)  21.1 us
    dot_general x1, matrix products, on_device_body(): jnp.dot(lax.all_gather(normed, TENSOR, axis=0, tiled=True), joined, prefe...  17.8 us
  transfers between devices with their start and end apart: 20, of which 12 were waited for; matrix products, arithmetic and copies ran while one was open for 12% of the time, Pallas kernels for 0%

profile of v3, /device:TPU:0, one launch (start us, length us, event | category | flops | bytes accessed | tf_op | source)
XLA Modules:
  0.0 385.3 jit_solution(12008070085466473227)
XLA Ops:
  7.2 1.7 fusion.27
  8.9 2.5 fusion.29
  11.6 0.1 add.274
  11.7 0.1 iota_add_fusion.1
  11.7 0.1 add.235
  11.8 3.1 dynamic-slice_bitcast_fusion.2
  14.9 3.1 iota_compare_fusion
  18.0 3.1 iota_compare_fusion.1
  21.1 84.5 %all-gather.2.cloned.1.call-done = bf16[2048,4096]{1,0:T(8,128)(2,1)} async-done(((bf16[128,4096]{1,0:T(8,128)(2,1)}), bf16[2048,4096]{1,0:T(8,128)(2,1)}) %all-gather.2.cloned.1.call-update) | async-done | bytes 16777232 | tf_op jit(solution)/shard_map/all_gather | solution.py:61
  105.6 17.8 %fusion.22 = bf16[2048,640]{0,1:T(8,128)(2,1)} fusion(bf16[2048,4096]{1,0:T(8,128)(2,1)} %all-gather.2.cloned.1.call-done, bf16[4096,256]{1,0:T(8,128)(2,1)} %dynamic-slice_bitcast_fusion.2, bf16[4096,384]{1,0:T(8,128)(2,1)} %bitcast.198), kind=kOutput, calls=%fused_computation.32 | convolution fusion | flops 10749214720 | bytes 24641536 | tf_op jit(solution)/shard_map/dot_general | solution.py:60
  123.4 2.3 slice.41
  125.7 1.5 slice_bitcast_fusion
  127.2 0.4 copy.19
  127.7 2.4 fusion.59
  130.0 2.6 copy.11
  132.7 2.6 copy.8
  135.3 12.5 %fusion.7 = (f32[3,1024]{1,0:T(4,128)S(1)}, f32[2048,1024,3]{1,0,2:T(8,128)}) fusion(pred[1024,2048]{0,1:T(8,128)(4,1)} %iota_compare_fusion, bf16[1024,3,128]{2,0,1:T(8,128)(2,1)} %bitcast.194, bf16[2048,1,2,128]{0,3,2,1:T(8,128)(2,1)} %bitcast.189), kind=kOutput, calls=%fused_computation.11 | convolution fusion | flops 1629484032 | bytes 28585984 | tf_op jit(solution)/shard_map/qkgd,skd->kgqs/dot_general | solution.py:90
  147.9 11.1 %fusion.5 = (f32[3,1024]{1,0:T(4,128)S(1)}, f32[2048,1024,3]{1,0,2:T(8,128)}) fusion(pred[1024,2048]{0,1:T(8,128)(4,1)S(1)} %copy-done.3, bf16[1024,3,128]{2,0,1:T(8,128)(2,1)S(1)} %bitcast.193, bf16[2048,1,2,128]{0,3,2,1:T(8,128)(2,1)S(1)} %bitcast.190), kind=kOutput, calls=%fused_computation.9 | convolution fusion | flops 1629484032 | bytes 28585984 | tf_op jit(solution)/shard_map/qkgd,skd->kgqs/dot_general | solution.py:90
  159.0 22.2 %fusion.4 = (f32[3]{0:T(128)S(1)}, f32[3,1024]{1,0:T(4,128)S(1)}, f32[3,1024]{1,0:T(4,128)S(1)}, f32[3]{0:T(128)S(1)}) fusion(f32[2048,1024,3]{1,0,2:T(8,128)} %get-tuple-element.25, pred[1024,2048]{0,1:T(8,128)(4,1)S(1)} %copy-done.3, f32[3,1024]{1,0:T(4,128)S(1)} %get-tuple-element.24, f32[3,1024]{1,0:T(4,128)S(1)} %get-tuple-element.26, ...), kind=kLoop, calls=%fused_computation.8 | loop fusion | flops 62908408 | bytes 54575128 | tf_op jit(solution)/shard_map/reduce_max | solution.py:106
  181.2 12.1 %fusion.30 = bf16[1024,1,3,128]{0,3,2,1:T(8,128)(2,1)S(1)} fusion(f32[2048,1024,3]{1,0,2:T(8,128)} %get-tuple-element.27, f32[3,1024]{1,0:T(4,128)S(1)} %get-tuple-element.26, pred[1024,2048]{0,1:T(8,128)(4,1)S(1)} %copy-done.4, f32[1024,3]{0,1:T(4,128)S(1)} %bitcast.197, bf16[2048,1,2,128]{0,3,2,1:T(8,128)(2,1)S(1)} %bitcast.191), kind=kOutput, calls=%fused_computation.43 | convolution fusion | flops 1636564992 | bytes 28606464 | tf_op jit(solution)/shard_map/kgqs,skd->qkgd/dot_general | solution.py:98
  193.4 4.8 %convolution_convert_fusion = bf16[1024,4096]{1,0:T(8,128)(2,1)S(1)} fusion(bf16[1024,384]{0,1:T(8,128)(2,1)S(1)} %bitcast.200, bf16[1,384,4096]{2,1,0:T(8,128)(2,1)S(1)} %copy-done), kind=kOutput, calls=%fused_computation.24 | convolution fusion | flops 3225419776 | bytes 12320768 | tf_op jit(solution)/shard_map/dot_general | solution.py:107
  198.2 3.2 copy-done.7
  201.5 2.5 dynamic-slice_bitcast_fusion
  203.9 0.3 collective-permute-start.9
  204.2 12.3 %fusion.31 = bf16[1024,1,3,128]{0,3,2,1:T(8,128)(2,1)S(1)} fusion(f32[2048,1024,3]{1,0,2:T(8,128)} %get-tuple-element.25, f32[3,1024]{1,0:T(4,128)S(1)} %get-tuple-element.24, pred[1024,2048]{0,1:T(8,128)(4,1)S(1)} %copy-done.3, f32[1024,3]{0,1:T(4,128)S(1)} %bitcast.196, bf16[2048,1,2,128]{0,3,2,1:T(8,128)(2,1)S(1)} %bitcast.192), kind=kOutput, calls=%fused_computation.45 | convolution fusion | flops 1636564992 | bytes 28606464 | tf_op jit(solution)/shard_map/kgqs,skd->qkgd/dot_general | solution.py:98
  216.5 4.8 %convolution_convert_fusion.1 = bf16[1024,4096]{1,0:T(8,128)(2,1)S(1)} fusion(bf16[1024,384]{0,1:T(8,128)(2,1)S(1)} %bitcast.199, bf16[1,384,4096]{2,1,0:T(8,128)(2,1)S(1)} %copy-done), kind=kOutput, calls=%fused_computation.25 | convolution fusion | flops 3225419776 | bytes 12320768 | tf_op jit(solution)/shard_map/dot_general | solution.py:107
  221.4 3.2 copy-done.5
  224.6 2.4 dynamic-slice_bitcast_fusion.1
  227.0 0.2 collective-permute-start
  227.3 5.2 %fusion.16 = bf16[8,64,4096]{2,1,0:T(8,128)(2,1)S(1)} fusion(bf16[8,64,4096]{2,1,0:T(8,128)(2,1)} %collective-permute-done.9, bf16[8,2,64,4096]{3,2,1,0:T(8,128)(2,1)} %bitcast.188, s32[]{:T(128)S(6)} %select_n.104), kind=kLoop, calls=%fused_computation.19 | loop fusion | flops 8388608 | bytes 12582916 | tf_op jit(solution)/shard_map/convert_element_type | solution.py:32
  232.5 1.6 dynamic-slice_bitcast_fusion.9
  234.1 1.3 collective-permute-start.10
  235.4 1.5 collective-permute-start.11
  236.9 2.3 collective-permute-start.12
  239.1 2.0 collective-permute-start.13
  241.2 2.4 collective-permute-start.14
  243.5 3.7 fusion.17
  247.3 1.7 dynamic-slice_bitcast_fusion.16
  249.0 1.0 copy-done.2
  250.0 1.2 collective-permute-done.10
  251.3 0.8 copy-done.10
  252.0 1.6 collective-permute-start.15
  253.6 19.5 %collective-permute-done.11 = bf16[64,4096]{1,0:T(8,128)(2,1)} collective-permute-done((bf16[64,4096]{1,0:T(8,128)(2,1)}, bf16[64,4096]{1,0:T(8,128)(2,1)}, u32[]{:S(2)}, u32[]{:S(2)}) %collective-permute-start.11) | collective-permute-done | bytes 524320 | tf_op jit(solution)/shard_map/ppermute | solution.py:38
  273.1 3.0 collective-permute-start.16
  276.0 10.4 %collective-permute-start.1 = (bf16[64,4096]{1,0:T(8,128)(2,1)S(1)}, bf16[64,4096]{1,0:T(8,128)(2,1)}, u32[]{:S(2)}, u32[]{:S(2)}) collective-permute-start(bf16[64,4096]{1,0:T(8,128)(2,1)S(1)} %get-tuple-element.6), channel_id=1, source_target_pairs={{0,2},{2,4},{4,6},{6,8},{8,10},{10,12},{12,14},{14,0},{1,3},{3,5},... | collective-permute-start | bytes 1572872 | tf_op jit(solution)/shard_map/ppermute | solution.py:38
  286.4 1.5 collective-permute-done.13
  287.9 5.4 %collective-permute-start.4 = (bf16[64,4096]{1,0:T(8,128)(2,1)}, bf16[64,4096]{1,0:T(8,128)(2,1)}, u32[]{:S(2)}, u32[]{:S(2)}) collective-permute-start(bf16[64,4096]{1,0:T(8,128)(2,1)} %get-tuple-element.10), channel_id=1, source_target_pairs={{0,8},{2,10},{4,12},{6,14},{8,0},{10,2},{12,4},{14,6},{1,9},{3,11}... | collective-permute-start | bytes 1572872 | tf_op jit(solution)/shard_map/ppermute | solution.py:38
  293.4 0.2 collective-permute-done.16
  293.6 3.9 %collective-permute-start.5 = (bf16[64,4096]{1,0:T(8,128)(2,1)}, bf16[64,4096]{1,0:T(8,128)(2,1)}, u32[]{:S(2)}, u32[]{:S(2)}) collective-permute-start(bf16[64,4096]{1,0:T(8,128)(2,1)} %get-tuple-element.9), channel_id=1, source_target_pairs={{0,10},{2,12},{4,14},{6,0},{8,2},{10,4},{12,6},{14,8},{1,11},{3,13... | collective-permute-start | bytes 1572872 | tf_op jit(solution)/shard_map/ppermute | solution.py:38
  297.5 3.1 collective-permute-done.1
  300.5 1.2 collective-permute-start.6
  301.8 19.4 %collective-permute-done.2 = bf16[64,4096]{1,0:T(8,128)(2,1)} collective-permute-done((bf16[64,4096]{1,0:T(8,128)(2,1)S(1)}, bf16[64,4096]{1,0:T(8,128)(2,1)}, u32[]{:S(2)}, u32[]{:S(2)}) %collective-permute-start.2) | collective-permute-done | bytes 524320 | tf_op jit(solution)/shard_map/ppermute | solution.py:38
  321.2 11.7 %collective-permute-start.7 = (bf16[64,4096]{1,0:T(8,128)(2,1)}, bf16[64,4096]{1,0:T(8,128)(2,1)}, u32[]{:S(2)}, u32[]{:S(2)}) collective-permute-start(bf16[64,4096]{1,0:T(8,128)(2,1)} %get-tuple-element.7), channel_id=1, source_target_pairs={{0,14},{2,0},{4,2},{6,4},{8,6},{10,8},{12,10},{14,12},{1,15},{3,1}... | collective-permute-start | bytes 1572872 | tf_op jit(solution)/shard_map/ppermute | solution.py:38
  332.9 2.8 convert_element_type.114
  335.7 4.8 %collective-permute-done.6 = bf16[64,4096]{1,0:T(8,128)(2,1)} collective-permute-done((bf16[64,4096]{1,0:T(8,128)(2,1)}, bf16[64,4096]{1,0:T(8,128)(2,1)}, u32[]{:S(2)}, u32[]{:S(2)}) %collective-permute-start.6) | collective-permute-done | bytes 524320 | tf_op jit(solution)/shard_map/ppermute | solution.py:38
  340.5 1.0 collective-permute-done.7
  341.5 5.4 %fusion.39 = (bf16[64,4096]{1,0:T(8,128)(2,1)S(1)}, bf16[64,4096]{1,0:T(8,128)(2,1)S(1)}) fusion(f32[1,1,128,4096]{3,2,1,0:T(8,128)} %convert_element_type.114, bf16[64,4096]{1,0:T(8,128)(2,1)} %collective-permute-done.7, bf16[64,4096]{1,0:T(8,128)(2,1)} %collective-permute-done.6, bf16[64,4096]{1,0:T(8,128)(2,1)} %collective-permute-done.5, ...), kind=kLoop, calls=%fused_computation.51 | loop fusion | flops 8912896 | bytes 11534340 | tf_op jit(solution)/shard_map/convert_element_type | solution.py:109
  346.9 8.5 %collective-permute-start.17 = (bf16[64,4096]{1,0:T(8,128)(2,1)S(1)}, bf16[64,4096]{1,0:T(8,128)(2,1)S(1)}, u32[]{:S(2)}, u32[]{:S(2)}) collective-permute-start(bf16[64,4096]{1,0:T(8,128)(2,1)S(1)} %get-tuple-element.21), channel_id=1, source_target_pairs={{48,0},{0,16},{16,32},{32,48},{49,1},{1,17},{17,33},{33,49},{50,2}... | collective-permute-start | bytes 1572872 | tf_op jit(solution)/shard_map/ppermute | solution.py:21
  355.4 0.1 collective-permute-start.8
  355.5 5.1 %collective-permute-done.18 = f32[1,3]{1,0:T(1,128)S(1)} collective-permute-done((f32[1,3]{1,0:T(1,128)S(1)}, f32[1,3]{1,0:T(1,128)S(1)}, u32[]{:S(2)}, u32[]{:S(2)}) %collective-permute-start.18) | collective-permute-done | bytes 44 | tf_op jit(solution)/shard_map/ppermute | solution.py:21
  360.5 0.5 max.3
  361.0 6.6 %collective-permute-done.17 = bf16[64,4096]{1,0:T(8,128)(2,1)S(1)} collective-permute-done((bf16[64,4096]{1,0:T(8,128)(2,1)S(1)}, bf16[64,4096]{1,0:T(8,128)(2,1)S(1)}, u32[]{:S(2)}, u32[]{:S(2)}) %collective-permute-start.17) | collective-permute-done | bytes 524320 | tf_op jit(solution)/shard_map/ppermute | solution.py:21
  367.7 9.4 %collective-permute-done.8 = bf16[64,4096]{1,0:T(8,128)(2,1)S(1)} collective-permute-done((bf16[64,4096]{1,0:T(8,128)(2,1)S(1)}, bf16[64,4096]{1,0:T(8,128)(2,1)S(1)}, u32[]{:S(2)}, u32[]{:S(2)}) %collective-permute-start.8) | collective-permute-done | bytes 524320 | tf_op jit(solution)/shard_map/ppermute | solution.py:21
  377.1 1.1 maximum_bitcast_fusion
  (36 shorter events, 0.2 us)
Async XLA Ops:
  7.2 186.2 %copy-start = (bf16[1,384,4096]{2,1,0:T(8,128)(2,1)S(1)}, bf16[1,384,4096]{2,1,0:T(8,128)(2,1)}, u32[]{:S(2)}) copy-start(bf16[1,384,4096]{2,1,0:T(8,128)(2,1)} %param.9) | copy-start | bytes 9437188
  7.2 98.5 %all-gather.2.cloned.1.call-start = ((), (), s32[]{:S(2)}) async-start(), calls=%async_computation | async-start | bytes 17825792 | tf_op jit(solution)/shard_map/all_gather | solution.py:61
  135.3 12.5 %copy-start.3 = (pred[1024,2048]{0,1:T(8,128)(4,1)S(1)}, pred[1024,2048]{0,1:T(8,128)(4,1)}, u32[]{:S(2)}) copy-start(pred[1024,2048]{0,1:T(8,128)(4,1)} %iota_compare_fusion.1) | copy-start | bytes 6291460
  135.3 12.5 %copy-start.8 = (bf16[2048,256]{0,1:T(8,128)(2,1)S(1)}, bf16[2048,256]{0,1:T(8,128)(2,1)}, u32[]{:S(2)}) copy-start(bf16[2048,256]{0,1:T(8,128)(2,1)} %slice.41) | copy-start | bytes 3145732
  135.3 12.5 %copy-start.9 = (bf16[16,64,1,3,128]{4,1,0,3,2:T(8,128)(2,1)S(1)}, bf16[16,64,1,3,128]{4,1,0,3,2:T(8,128)(2,1)}, u32[]{:S(2)}) copy-start(bf16[16,64,1,3,128]{4,1,0,3,2:T(8,128)(2,1)} %copy.8) | copy-start | bytes 2359300
  147.9 11.1 %copy-start.4 = (pred[1024,2048]{0,1:T(8,128)(4,1)S(1)}, pred[1024,2048]{0,1:T(8,128)(4,1)}, u32[]{:S(2)}) copy-start(pred[1024,2048]{0,1:T(8,128)(4,1)} %iota_compare_fusion) | copy-start | bytes 6291460
  198.2 3.2 copy-start.7
  203.9 23.4 %collective-permute-start.9 = (bf16[8,64,4096]{2,1,0:T(8,128)(2,1)}, bf16[8,64,4096]{2,1,0:T(8,128)(2,1)}, u32[]{:S(2)}, u32[]{:S(2)}) collective-permute-start(bf16[8,64,4096]{2,1,0:T(8,128)(2,1)} %dynamic-slice_bitcast_fusion), channel_id=1, source_target_pairs={{0,1},{1,0},{2,3},{3,2},{4,5},{5,4},{6,7},{7,6},{8,9},{9,8},{10,11... | collective-permute-start | bytes 12582920 | tf_op jit(solution)/shard_map/ppermute | solution.py:31
  221.4 3.2 copy-start.5
  227.0 14.1 %collective-permute-start = (bf16[8,64,4096]{2,1,0:T(8,128)(2,1)}, bf16[8,64,4096]{2,1,0:T(8,128)(2,1)}, u32[]{:S(2)}, u32[]{:S(2)}) collective-permute-start(bf16[8,64,4096]{2,1,0:T(8,128)(2,1)} %dynamic-slice_bitcast_fusion.1), channel_id=1, source_target_pairs={{0,1},{1,0},{2,3},{3,2},{4,5},{5,4},{6,7},{7,6},{8,9},{9,8},{10,11... | collective-permute-start | bytes 12582920 | tf_op jit(solution)/shard_map/ppermute | solution.py:31
  227.3 16.3 %copy-start.6 = (bf16[1024,4096]{1,0:T(8,128)(2,1)S(1)}, bf16[1024,4096]{1,0:T(8,128)(2,1)}, u32[]{:S(2)}) copy-start(bf16[1024,4096]{1,0:T(8,128)(2,1)} %copy-done.5) | copy-start | bytes 25165828
  232.5 14.8 %copy-start.1 = (bf16[8,64,4096]{2,1,0:T(8,128)(2,1)}, bf16[8,64,4096]{2,1,0:T(8,128)(2,1)S(1)}, u32[]{:S(2)}) copy-start(bf16[8,64,4096]{2,1,0:T(8,128)(2,1)S(1)} %fusion.16) | copy-start | bytes 12582916
  234.1 17.2 %collective-permute-start.10 = (bf16[64,4096]{1,0:T(8,128)(2,1)}, bf16[64,4096]{1,0:T(8,128)(2,1)S(1)}, u32[]{:S(2)}, u32[]{:S(2)}) collective-permute-start(bf16[64,4096]{1,0:T(8,128)(2,1)} %get-tuple-element.13), channel_id=1, source_target_pairs={{0,2},{2,4},{4,6},{6,8},{8,10},{10,12},{12,14},{14,0},{1,3},{3,5},... | collective-permute-start | bytes 1572872 | tf_op jit(solution)/shard_map/ppermute | solution.py:38
  235.4 37.7 %collective-permute-start.11 = (bf16[64,4096]{1,0:T(8,128)(2,1)}, bf16[64,4096]{1,0:T(8,128)(2,1)}, u32[]{:S(2)}, u32[]{:S(2)}) collective-permute-start(bf16[64,4096]{1,0:T(8,128)(2,1)} %get-tuple-element.19), channel_id=1, source_target_pairs={{0,4},{2,6},{4,8},{6,10},{8,12},{10,14},{12,0},{14,2},{1,5},{3,7},... | collective-permute-start | bytes 1572872 | tf_op jit(solution)/shard_map/ppermute | solution.py:38
  236.9 39.2 %collective-permute-start.12 = (bf16[64,4096]{1,0:T(8,128)(2,1)}, bf16[64,4096]{1,0:T(8,128)(2,1)}, u32[]{:S(2)}, u32[]{:S(2)}) collective-permute-start(bf16[64,4096]{1,0:T(8,128)(2,1)} %get-tuple-element.18), channel_id=1, source_target_pairs={{0,6},{2,8},{4,10},{6,12},{8,14},{10,0},{12,2},{14,4},{1,7},{3,9},... | collective-permute-start | bytes 1572872 | tf_op jit(solution)/shard_map/ppermute | solution.py:38
  239.1 48.8 %collective-permute-start.13 = (bf16[64,4096]{1,0:T(8,128)(2,1)S(1)}, bf16[64,4096]{1,0:T(8,128)(2,1)}, u32[]{:S(2)}, u32[]{:S(2)}) collective-permute-start(bf16[64,4096]{1,0:T(8,128)(2,1)S(1)} %get-tuple-element.17), channel_id=1, source_target_pairs={{0,8},{2,10},{4,12},{6,14},{8,0},{10,2},{12,4},{14,6},{1,9},{3,11}... | collective-permute-start | bytes 1572872 | tf_op jit(solution)/shard_map/ppermute | solution.py:38
  241.2 46.7 %collective-permute-start.14 = (bf16[64,4096]{1,0:T(8,128)(2,1)S(1)}, bf16[64,4096]{1,0:T(8,128)(2,1)}, u32[]{:S(2)}, u32[]{:S(2)}) collective-permute-start(bf16[64,4096]{1,0:T(8,128)(2,1)S(1)} %get-tuple-element.16), channel_id=1, source_target_pairs={{0,10},{2,12},{4,14},{6,0},{8,2},{10,4},{12,6},{14,8},{1,11},{3,13... | collective-permute-start | bytes 1572872 | tf_op jit(solution)/shard_map/ppermute | solution.py:38
  247.3 2.7 copy-start.2
  251.3 0.8 copy-start.10
  252.0 35.9 %collective-permute-start.15 = (bf16[64,4096]{1,0:T(8,128)(2,1)S(1)}, bf16[64,4096]{1,0:T(8,128)(2,1)}, u32[]{:S(2)}, u32[]{:S(2)}) collective-permute-start(bf16[64,4096]{1,0:T(8,128)(2,1)S(1)} %get-tuple-element.15), channel_id=1, source_target_pairs={{0,12},{2,14},{4,0},{6,2},{8,4},{10,6},{12,8},{14,10},{1,13},{3,15... | collective-permute-start | bytes 1572872 | tf_op jit(solution)/shard_map/ppermute | solution.py:38
  273.1 20.5 %collective-permute-start.16 = (bf16[64,4096]{1,0:T(8,128)(2,1)S(1)}, bf16[64,4096]{1,0:T(8,128)(2,1)}, u32[]{:S(2)}, u32[]{:S(2)}) collective-permute-start(bf16[64,4096]{1,0:T(8,128)(2,1)S(1)} %get-tuple-element.14), channel_id=1, source_target_pairs={{0,14},{2,0},{4,2},{6,4},{8,6},{10,8},{12,10},{14,12},{1,15},{3,1}... | collective-permute-start | bytes 1572872 | tf_op jit(solution)/shard_map/ppermute | solution.py:38
  276.0 24.5 %collective-permute-start.1 = (bf16[64,4096]{1,0:T(8,128)(2,1)S(1)}, bf16[64,4096]{1,0:T(8,128)(2,1)}, u32[]{:S(2)}, u32[]{:S(2)}) collective-permute-start(bf16[64,4096]{1,0:T(8,128)(2,1)S(1)} %get-tuple-element.6), channel_id=1, source_target_pairs={{0,2},{2,4},{4,6},{6,8},{8,10},{10,12},{12,14},{14,0},{1,3},{3,5},... | collective-permute-start | bytes 1572872 | tf_op jit(solution)/shard_map/ppermute | solution.py:38
  287.9 33.3 %collective-permute-start.2 = (bf16[64,4096]{1,0:T(8,128)(2,1)S(1)}, bf16[64,4096]{1,0:T(8,128)(2,1)}, u32[]{:S(2)}, u32[]{:S(2)}) collective-permute-start(bf16[64,4096]{1,0:T(8,128)(2,1)S(1)} %get-tuple-element.12), channel_id=1, source_target_pairs={{0,4},{2,6},{4,8},{6,10},{8,12},{10,14},{12,0},{14,2},{1,5},{3,7},... | collective-permute-start | bytes 1572872 | tf_op jit(solution)/shard_map/ppermute | solution.py:38
  287.9 47.8 %collective-permute-start.3 = (bf16[64,4096]{1,0:T(8,128)(2,1)}, bf16[64,4096]{1,0:T(8,128)(2,1)}, u32[]{:S(2)}, u32[]{:S(2)}) collective-permute-start(bf16[64,4096]{1,0:T(8,128)(2,1)} %get-tuple-element.11), channel_id=1, source_target_pairs={{0,6},{2,8},{4,10},{6,12},{8,14},{10,0},{12,2},{14,4},{1,7},{3,9},... | collective-permute-start | bytes 1572872 | tf_op jit(solution)/shard_map/ppermute | solution.py:38
  287.9 47.8 %collective-permute-start.4 = (bf16[64,4096]{1,0:T(8,128)(2,1)}, bf16[64,4096]{1,0:T(8,128)(2,1)}, u32[]{:S(2)}, u32[]{:S(2)}) collective-permute-start(bf16[64,4096]{1,0:T(8,128)(2,1)} %get-tuple-element.10), channel_id=1, source_target_pairs={{0,8},{2,10},{4,12},{6,14},{8,0},{10,2},{12,4},{14,6},{1,9},{3,11}... | collective-permute-start | bytes 1572872 | tf_op jit(solution)/shard_map/ppermute | solution.py:38
  293.6 42.1 %collective-permute-start.5 = (bf16[64,4096]{1,0:T(8,128)(2,1)}, bf16[64,4096]{1,0:T(8,128)(2,1)}, u32[]{:S(2)}, u32[]{:S(2)}) collective-permute-start(bf16[64,4096]{1,0:T(8,128)(2,1)} %get-tuple-element.9), channel_id=1, source_target_pairs={{0,10},{2,12},{4,14},{6,0},{8,2},{10,4},{12,6},{14,8},{1,11},{3,13... | collective-permute-start | bytes 1572872 | tf_op jit(solution)/shard_map/ppermute | solution.py:38
  300.5 40.0 %collective-permute-start.6 = (bf16[64,4096]{1,0:T(8,128)(2,1)}, bf16[64,4096]{1,0:T(8,128)(2,1)}, u32[]{:S(2)}, u32[]{:S(2)}) collective-permute-start(bf16[64,4096]{1,0:T(8,128)(2,1)} %get-tuple-element.8), channel_id=1, source_target_pairs={{0,12},{2,14},{4,0},{6,2},{8,4},{10,6},{12,8},{14,10},{1,13},{3,15... | collective-permute-start | bytes 1572872 | tf_op jit(solution)/shard_map/ppermute | solution.py:38
  321.2 20.3 %collective-permute-start.7 = (bf16[64,4096]{1,0:T(8,128)(2,1)}, bf16[64,4096]{1,0:T(8,128)(2,1)}, u32[]{:S(2)}, u32[]{:S(2)}) collective-permute-start(bf16[64,4096]{1,0:T(8,128)(2,1)} %get-tuple-element.7), channel_id=1, source_target_pairs={{0,14},{2,0},{4,2},{6,4},{8,6},{10,8},{12,10},{14,12},{1,15},{3,1}... | collective-permute-start | bytes 1572872 | tf_op jit(solution)/shard_map/ppermute | solution.py:38
  346.9 20.8 %collective-permute-start.17 = (bf16[64,4096]{1,0:T(8,128)(2,1)S(1)}, bf16[64,4096]{1,0:T(8,128)(2,1)S(1)}, u32[]{:S(2)}, u32[]{:S(2)}) collective-permute-start(bf16[64,4096]{1,0:T(8,128)(2,1)S(1)} %get-tuple-element.21), channel_id=1, source_target_pairs={{48,0},{0,16},{16,32},{32,48},{49,1},{1,17},{17,33},{33,49},{50,2}... | collective-permute-start | bytes 1572872 | tf_op jit(solution)/shard_map/ppermute | solution.py:21
  355.4 21.7 %collective-permute-start.8 = (bf16[64,4096]{1,0:T(8,128)(2,1)S(1)}, bf16[64,4096]{1,0:T(8,128)(2,1)S(1)}, u32[]{:S(2)}, u32[]{:S(2)}) collective-permute-start(bf16[64,4096]{1,0:T(8,128)(2,1)S(1)} %get-tuple-element.20), channel_id=1, source_target_pairs={{48,0},{0,16},{16,32},{32,48},{49,1},{1,17},{17,33},{33,49},{50,2}... | collective-permute-start | bytes 1572872 | tf_op jit(solution)/shard_map/ppermute | solution.py:21
  355.5 5.1 %collective-permute-start.18 = (f32[1,3]{1,0:T(1,128)S(1)}, f32[1,3]{1,0:T(1,128)S(1)}, u32[]{:S(2)}, u32[]{:S(2)}) collective-permute-start(f32[1,3]{1,0:T(1,128)S(1)} %maximum_bitcast_fusion.1), channel_id=1, source_target_pairs={{64,0},{0,64},{65,1},{1,65},{66,2},{2,66},{67,3},{3,67},{68,4},{4,... | collective-permute-start | bytes 44 | tf_op jit(solution)/shard_map/ppermute | solution.py:21
Sparse Core Ops, SparseCore 0:
  11.6 94.0 all-gather.1

commit v4 on v3

--- a/solution.py
+++ b/solution.py
@@ -12,7 +12,7 @@
 CHIPS = ("ty", "tx")
 CORE = "tc"
 TENSOR = CHIPS + (CORE,)
-N_BLOCKS = 2
+N_BLOCKS = 4
 
 
 def from_behind(block, axis, distance):
@@ -22,20 +22,26 @@
 
 
 def scatter_sum(partial):
-    n_chips = lax.axis_size(CHIPS)
-    rows = partial.shape[0] // (2 * n_chips)
+    n_y = lax.axis_size("ty")
+    rows = partial.shape[0] // (4 * n_y)
+    cols = partial.shape[1]
     core = lax.axis_index(CORE)
-    halves = partial.reshape(n_chips, 2, rows, partial.shape[1])
-    keep = lax.dynamic_index_in_dim(halves, core, 1, keepdims=False)
-    give = lax.dynamic_index_in_dim(halves, 1 - core, 1, keepdims=False)
+    halves = partial.reshape(n_y, 2, 2, rows, cols)
+    keep = lax.dynamic_index_in_dim(halves, core, 2, keepdims=False)
+    give = lax.dynamic_index_in_dim(halves, 1 - core, 2, keepdims=False)
     got = lax.ppermute(give, CORE, [(0, 1), (1, 0)])
     pair = (keep.astype(jnp.float32) + got.astype(jnp.float32)).astype(jnp.bfloat16)
-    chip = lax.axis_index(CHIPS)
-    total = lax.dynamic_index_in_dim(pair, chip, 0, keepdims=False).astype(jnp.float32)
-    for k in range(1, n_chips):
-        send = lax.dynamic_index_in_dim(pair, (chip + k) % n_chips, 0, keepdims=False)
-        route = [(i, (i + k) % n_chips) for i in range(n_chips)]
-        got = lax.ppermute(send, CHIPS, route)
+    x_pos = lax.axis_index("tx")
+    keep = lax.dynamic_index_in_dim(pair, x_pos, 1, keepdims=False)
+    give = lax.dynamic_index_in_dim(pair, 1 - x_pos, 1, keepdims=False)
+    got = lax.ppermute(give, "tx", [(0, 1), (1, 0)])
+    quad = (keep.astype(jnp.float32) + got.astype(jnp.float32)).astype(jnp.bfloat16)
+    y_pos = lax.axis_index("ty")
+    total = lax.dynamic_index_in_dim(quad, y_pos, 0, keepdims=False).astype(jnp.float32)
+    for k in range(1, n_y):
+        send = lax.dynamic_index_in_dim(quad, (y_pos + k) % n_y, 0, keepdims=False)
+        route = [(i, (i + k) % n_y) for i in range(n_y)]
+        got = lax.ppermute(send, "ty", route)
         total = total + got.astype(jnp.float32)
     return total
 

time: 390 us -> 381 us (0.977)
  waiting for transfers between devices: 156 us -> 196 us
  starting transfers between devices: 55.7 us -> 32.5 us
  matrix products: 75.5 us -> 59.7 us
  other arithmetic: 51.5 us -> 42.2 us
    ppermute x14 -> x16, waiting for transfers between devices: 50.7 us -> 100 us  [the longest x4 75.1 us: scatter_sum(): got = lax.ppermute(give, 'tx', [(0, 1), (1, 0)])]
    ppermute x14 -> x16, starting transfers between devices: 46.6 us -> 22.3 us  [the longest x12 17.9 us: scatter_sum(): got = lax.ppermute(send, 'ty', route)]
    dynamic_slice x0 -> x6, local copies, waits for them, and re-layouts: none -> 10.4 us  [the longest x2 5.48 us: scatter_sum(): keep = lax.dynamic_index_in_dim(halves, core, 2, keepdims=False)]
    ppermute x3 -> x5, waiting for transfers between devices: 21.1 us -> 12.7 us  [from_behind(): return lax.ppermute(block, axis, route)]
    unnamed x24 -> x38, local copies, waits for them, and re-layouts: 10.2 us -> 2.14 us
    dot_general x2 -> x4, matrix products: 24.4 us -> 16.7 us  [on_device_body(): jnp.einsum('kgqs,skd->qkgd', expw.astype(jnp.bfloat16), value_heads, pref...]
    squeeze x4 -> x8, local copies, waits for them, and re-layouts: 8.25 us -> 0.62 us  [the longest x4 0.38 us: scatter_sum(): give = lax.dynamic_index_in_dim(pair, 1 - x_pos, 1, keepdims=False)]
    dot_general x2 -> x4, matrix products: 23.6 us -> 16.1 us  [on_device_body(): jnp.einsum('qkgd,skd->kgqs', query_block, key_heads, preferred_element_ty...]
  transfers between devices with their start and end apart: 20 -> 26, of which waited for: 12 -> 15; matrix products, arithmetic and copies ran while one was open for 12% -> 17% of each run, Pallas kernels for 0% -> 0%
where the time goes in v4:
time: 381 us; the launch traced here: 376 us
  waiting for transfers between devices  196 us (51%)
  matrix products  59.7 us (16%)
  other arithmetic  42.2 us (11%)
  starting transfers between devices  32.5 us (9%)
  local copies, waits for them, and re-layouts  31.1 us (8%)
  between operations  14.8 us (4%)
    all_gather x1, waiting for transfers between devices, on_device_body(): lax.all_gather(normed, TENSOR, axis=0, tiled=True)  83.2 us
    ppermute x4, waiting for transfers between devices, scatter_sum(): got = lax.ppermute(give, 'tx', [(0, 1), (1, 0)])  75.1 us
    ppermute x12, waiting for transfers between devices, scatter_sum(): got = lax.ppermute(send, 'ty', route)  25.1 us
    reduce_max x4, other arithmetic, on_device_body(): peaks.append(jnp.max(row_max[..., 0], axis=2))  19 us
    ppermute x12, starting transfers between devices, scatter_sum(): got = lax.ppermute(send, 'ty', route)  17.9 us
    dot_general x1, matrix products, on_device_body(): jnp.dot(lax.all_gather(normed, TENSOR, axis=0, tiled=True), joined, prefe...  17.4 us
    dot_general x4, matrix products, on_device_body(): jnp.einsum('kgqs,skd->qkgd', expw.astype(jnp.bfloat16), value_heads, pref...  16.7 us
    dot_general x4, matrix products, on_device_body(): jnp.einsum('qkgd,skd->kgqs', query_block, key_heads, preferred_element_ty...  16.1 us
  transfers between devices with their start and end apart: 26, of which 15 were waited for; matrix products, arithmetic and copies ran while one was open for 17% of the time, Pallas kernels for 0%

profile of v4, /device:TPU:0, one launch (start us, length us, event | category | flops | bytes accessed | tf_op | source)
XLA Modules:
  0.0 376.4 jit_solution(7618776160829046688)
XLA Ops:
  7.2 1.7 fusion.51
  8.9 2.6 fusion.53
  12.2 1.8 iota_compare_fusion
  14.0 1.8 iota_compare_fusion.1
  15.8 1.8 iota_compare_fusion.2
  17.6 1.8 iota_compare_fusion.3
  19.4 3.1 dynamic-slice_bitcast_fusion
  22.5 83.2 %all-gather.2.cloned.1.call-done = bf16[2048,4096]{1,0:T(8,128)(2,1)} async-done(((bf16[128,4096]{1,0:T(8,128)(2,1)}), bf16[2048,4096]{1,0:T(8,128)(2,1)}) %all-gather.2.cloned.1.call-update) | async-done | bytes 16777232 | tf_op jit(solution)/shard_map/all_gather | solution.py:67
  105.7 17.4 %fusion.40 = bf16[2048,640]{0,1:T(8,128)(2,1)} fusion(bf16[2048,4096]{1,0:T(8,128)(2,1)} %all-gather.2.cloned.1.call-done, bf16[4096,256]{1,0:T(8,128)(2,1)} %dynamic-slice_bitcast_fusion, bf16[4096,384]{1,0:T(8,128)(2,1)} %bitcast.394), kind=kOutput, calls=%fused_computation.56 | convolution fusion | flops 10749214720 | bytes 24641536 | tf_op jit(solution)/shard_map/dot_general | solution.py:66
  123.1 1.5 slice_bitcast_fusion
  124.6 2.3 slice.65
  127.3 4.1 %fusion.119 = (bf16[16,32,1,3,128]{1,0,4,3,2:T(8,128)(2,1)}, bf16[16,32,1,3,128]{1,0,4,3,2:T(8,128)(2,1)}, bf16[16,32,1,3,128]{1,0,4,3,2:T(8,128)(2,1)}, bf16[16,32,1,3,128]{1,0,4,3,2:T(8,128)(2,1)}) fusion(bf16[16,128,1,3,128]{1,0,4,3,2:T(8,128)(2,1)S(1)} %bitcast.366), kind=kLoop, calls=%fused_computation.170 | loop fusion | bytes 3145728 | tf_op jit(solution)/shard_map/slice | solution.py:89
  131.5 1.9 copy.20
  133.4 4.0 %fusion.15 = (f32[3,512]{1,0:T(4,128)S(1)}, f32[2048,512,3]{1,0,2:T(8,128)S(1)}) fusion(pred[512,2048]{0,1:T(8,128)(4,1)} %iota_compare_fusion, bf16[512,3,128]{2,0,1:T(8,128)(2,1)S(1)} %bitcast.381, bf16[2048,1,2,128]{0,3,2,1:T(8,128)(2,1)} %bitcast.373), kind=kOutput, calls=%fused_computation.23 | convolution fusion | flops 814742016 | bytes 14555136 | tf_op jit(solution)/shard_map/qkgd,skd->kgqs/dot_general | solution.py:96
  137.5 4.7 %fusion.14 = (f32[3]{0:T(128)S(1)}, f32[3,512]{1,0:T(4,128)S(1)}) fusion(f32[2048,512,3]{1,0,2:T(8,128)S(1)} %get-tuple-element.38, pred[512,2048]{0,1:T(8,128)(4,1)S(1)} %copy-done.11, f32[3,512]{1,0:T(4,128)S(1)} %get-tuple-element.37), kind=kLoop, calls=%fused_computation.22 | loop fusion | flops 15727101 | bytes 13643788 | tf_op jit(solution)/shard_map/reduce_max | solution.py:112
  142.2 4.6 %fusion.87 = bf16[512,1,3,128]{0,3,2,1:T(8,128)(2,1)} fusion(f32[2048,512,3]{1,0,2:T(8,128)S(1)} %get-tuple-element.38, f32[3,512]{1,0:T(4,128)S(1)} %get-tuple-element.37, pred[512,2048]{0,1:T(8,128)(4,1)S(1)} %copy-done.11, f32[512,3]{0,1:T(4,128)S(1)} %bitcast.391, bf16[2048,1,2,128]{0,3,2,1:T(8,128)(2,1)S(1)} %bitcast.377), kind=kOutput, calls=%fused_computation.100 | convolution fusion | flops 818282496 | bytes 14565376 | tf_op jit(solution)/shard_map/kgqs,skd->qkgd/dot_general | solution.py:104
  146.8 1.9 copy.16
  148.8 4.0 %fusion.13 = (f32[3,512]{1,0:T(4,128)S(1)}, f32[2048,512,3]{1,0,2:T(8,128)S(1)}) fusion(pred[512,2048]{0,1:T(8,128)(4,1)} %iota_compare_fusion.1, bf16[512,3,128]{2,0,1:T(8,128)(2,1)S(1)} %bitcast.382, bf16[2048,1,2,128]{0,3,2,1:T(8,128)(2,1)} %bitcast.374), kind=kOutput, calls=%fused_computation.21 | convolution fusion | flops 814742016 | bytes 14555136 | tf_op jit(solution)/shard_map/qkgd,skd->kgqs/dot_general | solution.py:96
  152.8 4.7 %fusion.12 = (f32[3]{0:T(128)S(1)}, f32[3,512]{1,0:T(4,128)S(1)}) fusion(f32[2048,512,3]{1,0,2:T(8,128)S(1)} %get-tuple-element.42, pred[512,2048]{0,1:T(8,128)(4,1)S(1)} %copy-done.10, f32[3,512]{1,0:T(4,128)S(1)} %get-tuple-element.41), kind=kLoop, calls=%fused_computation.20 | loop fusion | flops 15727101 | bytes 13643788 | tf_op jit(solution)/shard_map/reduce_max | solution.py:112
  157.6 3.7 fusion.81
  161.4 2.4 convolution_convert_fusion
  163.7 2.4 convolution_convert_fusion.1
  166.1 2.7 constant_dynamic-slice_fusion.1
  168.9 1.5 copy.50
  170.7 2.3 copy.12
  173.0 4.0 %fusion.11 = (f32[3,512]{1,0:T(4,128)S(1)}, f32[2048,512,3]{1,0,2:T(8,128)S(1)}) fusion(pred[512,2048]{0,1:T(8,128)(4,1)} %iota_compare_fusion.2, bf16[512,3,128]{2,0,1:T(8,128)(2,1)S(1)} %bitcast.383, bf16[2048,1,2,128]{0,3,2,1:T(8,128)(2,1)} %bitcast.375), kind=kOutput, calls=%fused_computation.19 | convolution fusion | flops 814742016 | bytes 14555136 | tf_op jit(solution)/shard_map/qkgd,skd->kgqs/dot_general | solution.py:96
  177.0 4.7 %fusion.10 = (f32[3]{0:T(128)S(1)}, f32[3,512]{1,0:T(4,128)S(1)}) fusion(f32[2048,512,3]{1,0,2:T(8,128)S(1)} %get-tuple-element.44, pred[512,2048]{0,1:T(8,128)(4,1)S(1)} %copy-done.9, f32[3,512]{1,0:T(4,128)S(1)} %get-tuple-element.43), kind=kLoop, calls=%fused_computation.18 | loop fusion | flops 15727101 | bytes 13643788 | tf_op jit(solution)/shard_map/reduce_max | solution.py:112
  181.8 4.4 %fusion.75 = bf16[512,1,3,128]{0,3,2,1:T(8,128)(2,1)} fusion(f32[2048,512,3]{1,0,2:T(8,128)S(1)} %get-tuple-element.44, f32[3,512]{1,0:T(4,128)S(1)} %get-tuple-element.43, pred[512,2048]{0,1:T(8,128)(4,1)S(1)} %copy-done.9, f32[512,3]{0,1:T(4,128)S(1)} %bitcast.393, bf16[2048,1,2,128]{0,3,2,1:T(8,128)(2,1)S(1)} %bitcast.379), kind=kOutput, calls=%fused_computation.96 | convolution fusion | flops 818282496 | bytes 14565376 | tf_op jit(solution)/shard_map/kgqs,skd->qkgd/dot_general | solution.py:104
  186.2 1.9 copy.8
  188.1 4.0 %fusion.9 = (f32[3,512]{1,0:T(4,128)S(1)}, f32[2048,512,3]{1,0,2:T(8,128)S(1)}) fusion(pred[512,2048]{0,1:T(8,128)(4,1)} %iota_compare_fusion.3, bf16[512,3,128]{2,0,1:T(8,128)(2,1)S(1)} %bitcast.384, bf16[2048,1,2,128]{0,3,2,1:T(8,128)(2,1)} %bitcast.376), kind=kOutput, calls=%fused_computation.17 | convolution fusion | flops 814742016 | bytes 14555136 | tf_op jit(solution)/shard_map/qkgd,skd->kgqs/dot_general | solution.py:96
  192.2 4.7 %fusion.8 = (f32[3]{0:T(128)S(1)}, f32[3,512]{1,0:T(4,128)S(1)}) fusion(f32[2048,512,3]{1,0,2:T(8,128)S(1)} %get-tuple-element.40, pred[512,2048]{0,1:T(8,128)(4,1)S(1)} %copy-done.8, f32[3,512]{1,0:T(4,128)S(1)} %get-tuple-element.39), kind=kLoop, calls=%fused_computation.16 | loop fusion | flops 15727101 | bytes 13643788 | tf_op jit(solution)/shard_map/reduce_max | solution.py:112
  197.0 3.9 %fusion.69 = bf16[512,1,3,128]{0,3,2,1:T(8,128)(2,1)S(1)} fusion(f32[2048,512,3]{1,0,2:T(8,128)S(1)} %get-tuple-element.40, f32[3,512]{1,0:T(4,128)S(1)} %get-tuple-element.39, pred[512,2048]{0,1:T(8,128)(4,1)S(1)} %copy-done.8, f32[512,3]{0,1:T(4,128)S(1)} %bitcast.390, bf16[2048,1,2,128]{0,3,2,1:T(8,128)(2,1)S(1)} %bitcast.380), kind=kOutput, calls=%fused_computation.94 | convolution fusion | flops 818282496 | bytes 14565376 | tf_op jit(solution)/shard_map/kgqs,skd->qkgd/dot_general | solution.py:104
  200.9 2.4 convolution_convert_fusion.2
  203.3 2.4 convolution_convert_fusion.3
  205.6 2.7 constant_dynamic-slice_fusion.5
  208.4 1.4 copy.53
  210.1 1.5 convert_element_type.216
  211.6 1.9 copy.51
  214.5 2.5 fusion.36
  218.5 2.5 fusion.39
  222.8 1.4 collective-permute-start.13
  225.9 17.3 %collective-permute-done.19 = bf16[4,32,4096]{2,1,0:T(8,128)(2,1)S(1)} collective-permute-done((bf16[4,32,4096]{2,1,0:T(8,128)(2,1)S(1)}, bf16[4,32,4096]{2,1,0:T(8,128)(2,1)S(1)}, u32[]{:S(2)}, u32[]{:S(2)}) %collective-permute-start.19) | collective-permute-done | bytes 1048608 | tf_op jit(solution)/shard_map/ppermute | solution.py:37
  243.5 2.8 collective-permute-start.22
  247.1 18.5 %collective-permute-done.1 = bf16[4,32,4096]{2,1,0:T(8,128)(2,1)S(1)} collective-permute-done((bf16[4,32,4096]{2,1,0:T(8,128)(2,1)S(1)}, bf16[4,32,4096]{2,1,0:T(8,128)(2,1)S(1)}, u32[]{:S(2)}, u32[]{:S(2)}) %collective-permute-start.1) | collective-permute-done | bytes 1048608 | tf_op jit(solution)/shard_map/ppermute | solution.py:37
  265.7 1.7 collective-permute-start.20
  267.7 20.5 %collective-permute-done.13 = bf16[4,32,4096]{2,1,0:T(8,128)(2,1)S(1)} collective-permute-done((bf16[4,32,4096]{2,1,0:T(8,128)(2,1)S(1)}, bf16[4,32,4096]{2,1,0:T(8,128)(2,1)S(1)}, u32[]{:S(2)}, u32[]{:S(2)}) %collective-permute-start.13) | collective-permute-done | bytes 1048608 | tf_op jit(solution)/shard_map/ppermute | solution.py:37
  288.1 2.7 collective-permute-start.4
  291.1 18.8 %collective-permute-done.7 = bf16[4,32,4096]{2,1,0:T(8,128)(2,1)S(1)} collective-permute-done((bf16[4,32,4096]{2,1,0:T(8,128)(2,1)S(1)}, bf16[4,32,4096]{2,1,0:T(8,128)(2,1)S(1)}, u32[]{:S(2)}, u32[]{:S(2)}) %collective-permute-start.7) | collective-permute-done | bytes 1048608 | tf_op jit(solution)/shard_map/ppermute | solution.py:37
  309.9 2.7 collective-permute-start.3
  313.9 2.4 collective-permute-start.16
  317.5 3.1 collective-permute-done.3
  320.6 2.7 collective-permute-start.10
  323.3 5.7 %collective-permute-done.2 = bf16[32,4096]{1,0:T(8,128)(2,1)S(1)} collective-permute-done((bf16[32,4096]{1,0:T(8,128)(2,1)S(1)}, bf16[32,4096]{1,0:T(8,128)(2,1)S(1)}, u32[]{:S(2)}, u32[]{:S(2)}) %collective-permute-start.2) | collective-permute-done | bytes 262176 | tf_op jit(solution)/shard_map/ppermute | solution.py:44
  329.2 2.7 collective-permute-done.15
  331.8 1.6 collective-permute-start.23
  333.4 6.8 %collective-permute-done.14 = bf16[32,4096]{1,0:T(8,128)(2,1)S(1)} collective-permute-done((bf16[32,4096]{1,0:T(8,128)(2,1)S(1)}, bf16[32,4096]{1,0:T(8,128)(2,1)S(1)}, u32[]{:S(2)}, u32[]{:S(2)}) %collective-permute-start.14) | collective-permute-done | bytes 262176 | tf_op jit(solution)/shard_map/ppermute | solution.py:44
  340.2 3.0 collective-permute-done.9
  343.1 4.0 %collective-permute-done.8 = bf16[32,4096]{1,0:T(8,128)(2,1)S(1)} collective-permute-done((bf16[32,4096]{1,0:T(8,128)(2,1)S(1)}, bf16[32,4096]{1,0:T(8,128)(2,1)S(1)}, u32[]{:S(2)}, u32[]{:S(2)}) %collective-permute-start.8) | collective-permute-done | bytes 262176 | tf_op jit(solution)/shard_map/ppermute | solution.py:44
  347.6 1.6 collective-permute-start.17
  349.3 1.6 collective-permute-start.11
  352.1 3.0 collective-permute-start.24
  355.1 2.1 collective-permute-done.24
  358.1 5.6 %collective-permute-done.11 = bf16[32,4096]{1,0:T(8,128)(2,1)S(1)} collective-permute-done((bf16[32,4096]{1,0:T(8,128)(2,1)S(1)}, bf16[32,4096]{1,0:T(8,128)(2,1)S(1)}, u32[]{:S(2)}, u32[]{:S(2)}) %collective-permute-start.11) | collective-permute-done | bytes 262176 | tf_op jit(solution)/shard_map/ppermute | solution.py:21
  363.7 4.6 %collective-permute-done.5 = bf16[32,4096]{1,0:T(8,128)(2,1)S(1)} collective-permute-done((bf16[32,4096]{1,0:T(8,128)(2,1)S(1)}, bf16[32,4096]{1,0:T(8,128)(2,1)S(1)}, u32[]{:S(2)}, u32[]{:S(2)}) %collective-permute-start.5) | collective-permute-done | bytes 262176 | tf_op jit(solution)/shard_map/ppermute | solution.py:21
  (98 shorter events, 15.7 us)
Async XLA Ops:
  7.2 154.2 %copy-start = (bf16[1,384,4096]{2,1,0:T(8,128)(2,1)S(1)}, bf16[1,384,4096]{2,1,0:T(8,128)(2,1)}, u32[]{:S(2)}) copy-start(bf16[1,384,4096]{2,1,0:T(8,128)(2,1)} %param.9) | copy-start | bytes 9437188
  7.2 98.5 %all-gather.2.cloned.1.call-start = ((), (), s32[]{:S(2)}) async-start(), calls=%async_computation | async-start | bytes 17825792 | tf_op jit(solution)/shard_map/all_gather | solution.py:67
  133.4 4.1 %copy-start.11 = (pred[512,2048]{0,1:T(8,128)(4,1)S(1)}, pred[512,2048]{0,1:T(8,128)(4,1)}, u32[]{:S(2)}) copy-start(pred[512,2048]{0,1:T(8,128)(4,1)} %iota_compare_fusion) | copy-start | bytes 3145732
  137.5 4.8 %copy-start.12 = (bf16[2048,256]{0,1:T(8,128)(2,1)S(1)}, bf16[2048,256]{0,1:T(8,128)(2,1)}, u32[]{:S(2)}) copy-start(bf16[2048,256]{0,1:T(8,128)(2,1)} %slice.65) | copy-start | bytes 3145732
  148.8 4.1 %copy-start.10 = (pred[512,2048]{0,1:T(8,128)(4,1)S(1)}, pred[512,2048]{0,1:T(8,128)(4,1)}, u32[]{:S(2)}) copy-start(pred[512,2048]{0,1:T(8,128)(4,1)} %iota_compare_fusion.1) | copy-start | bytes 3145732
  152.8 4.8 %copy-start.13 = (bf16[2048,256]{0,1:T(8,128)(2,1)S(1)}, bf16[2048,256]{0,1:T(8,128)(2,1)}, u32[]{:S(2)}) copy-start(bf16[2048,256]{0,1:T(8,128)(2,1)} %slice.65) | copy-start | bytes 3145732
  157.6 3.8 %copy-start.17 = (bf16[512,1,3,128]{0,3,2,1:T(8,128)(2,1)S(1)}, bf16[512,1,3,128]{0,3,2,1:T(8,128)(2,1)}, u32[]{:S(2)}) copy-start(bf16[512,1,3,128]{0,3,2,1:T(8,128)(2,1)} %fusion.87) | copy-start | bytes 1179652
  170.4 43.9 %collective-permute-start.18 = (bf16[4,2,32,4096]{3,2,0,1:T(8,128)(2,1)}, bf16[4,2,32,4096]{3,2,0,1:T(8,128)(2,1)}, u32[]{:S(2)}, u32[]{:S(2)}) collective-permute-start(bf16[4,2,32,4096]{3,2,0,1:T(8,128)(2,1)} %bitcast.362), channel_id=1, source_target_pairs={{0,1},{1,0},{2,3},{3,2},{4,5},{5,4},{6,7},{7,6},{8,9},{9,8},{10,11... | collective-permute-start | bytes 6291464 | tf_op jit(solution)/shard_map/ppermute | solution.py:32
  173.0 4.1 %copy-start.9 = (pred[512,2048]{0,1:T(8,128)(4,1)S(1)}, pred[512,2048]{0,1:T(8,128)(4,1)}, u32[]{:S(2)}) copy-start(pred[512,2048]{0,1:T(8,128)(4,1)} %iota_compare_fusion.2) | copy-start | bytes 3145732
  177.0 4.8 %copy-start.14 = (bf16[2048,256]{0,1:T(8,128)(2,1)S(1)}, bf16[2048,256]{0,1:T(8,128)(2,1)}, u32[]{:S(2)}) copy-start(bf16[2048,256]{0,1:T(8,128)(2,1)} %slice.65) | copy-start | bytes 3145732
  188.1 4.1 %copy-start.8 = (pred[512,2048]{0,1:T(8,128)(4,1)S(1)}, pred[512,2048]{0,1:T(8,128)(4,1)}, u32[]{:S(2)}) copy-start(pred[512,2048]{0,1:T(8,128)(4,1)} %iota_compare_fusion.3) | copy-start | bytes 3145732
  192.2 4.8 %copy-start.15 = (bf16[2048,256]{0,1:T(8,128)(2,1)S(1)}, bf16[2048,256]{0,1:T(8,128)(2,1)}, u32[]{:S(2)}) copy-start(bf16[2048,256]{0,1:T(8,128)(2,1)} %slice.65) | copy-start | bytes 3145732
  196.9 3.9 %copy-start.16 = (bf16[512,1,3,128]{0,3,2,1:T(8,128)(2,1)S(1)}, bf16[512,1,3,128]{0,3,2,1:T(8,128)(2,1)}, u32[]{:S(2)}) copy-start(bf16[512,1,3,128]{0,3,2,1:T(8,128)(2,1)} %fusion.75) | copy-start | bytes 1179652
  208.4 1.7 copy-start.1
  209.8 8.7 %collective-permute-start = (bf16[4,2,32,4096]{3,2,0,1:T(8,128)(2,1)}, bf16[4,2,32,4096]{3,2,0,1:T(8,128)(2,1)}, u32[]{:S(2)}, u32[]{:S(2)}) collective-permute-start(bf16[4,2,32,4096]{3,2,0,1:T(8,128)(2,1)} %bitcast.365), channel_id=1, source_target_pairs={{0,1},{1,0},{2,3},{3,2},{4,5},{5,4},{6,7},{7,6},{8,9},{9,8},{10,11... | collective-permute-start | bytes 6291464 | tf_op jit(solution)/shard_map/ppermute | solution.py:32
  211.6 2.2 copy-start.6
  211.6 2.9 copy-start.3
  213.5 8.4 %collective-permute-start.12 = (bf16[4,2,32,4096]{3,2,0,1:T(8,128)(2,1)S(1)}, bf16[4,2,32,4096]{3,2,0,1:T(8,128)(2,1)S(1)}, u32[]{:S(2)}, u32[]{:S(2)}) collective-permute-start(bf16[4,2,32,4096]{3,2,0,1:T(8,128)(2,1)S(1)} %bitcast.372), channel_id=1, source_target_pairs={{0,1},{1,0},{2,3},{3,2},{4,5},{5,4},{6,7},{7,6},{8,9},{9,8},{10,11... | collective-permute-start | bytes 6291464 | tf_op jit(solution)/shard_map/ppermute | solution.py:32
  214.0 10.2 %collective-permute-start.6 = (bf16[4,2,32,4096]{3,2,0,1:T(8,128)(2,1)S(1)}, bf16[4,2,32,4096]{3,2,0,1:T(8,128)(2,1)S(1)}, u32[]{:S(2)}, u32[]{:S(2)}) collective-permute-start(bf16[4,2,32,4096]{3,2,0,1:T(8,128)(2,1)S(1)} %bitcast.371), channel_id=1, source_target_pairs={{0,1},{1,0},{2,3},{3,2},{4,5},{5,4},{6,7},{7,6},{8,9},{9,8},{10,11... | collective-permute-start | bytes 6291464 | tf_op jit(solution)/shard_map/ppermute | solution.py:32
  214.4 4.0 %copy-start.5 = (bf16[4,2,1,32,4096]{4,3,2,1,0:T(8,128)(2,1)S(1)}, bf16[4,2,1,32,4096]{4,3,2,1,0:T(8,128)(2,1)}, u32[]{:S(2)}) copy-start(bf16[4,2,1,32,4096]{4,3,2,1,0:T(8,128)(2,1)} %get-tuple-element.48) | copy-start | bytes 6291460
  217.1 26.1 %collective-permute-start.19 = (bf16[4,32,4096]{2,1,0:T(8,128)(2,1)S(1)}, bf16[4,32,4096]{2,1,0:T(8,128)(2,1)S(1)}, u32[]{:S(2)}, u32[]{:S(2)}) collective-permute-start(bf16[4,32,4096]{2,1,0:T(8,128)(2,1)S(1)} %dynamic-slice_bitcast_fusion.1), channel_id=1, source_target_pairs={{0,2},{2,0},{1,3},{3,1},{4,6},{6,4},{5,7},{7,5},{8,10},{10,8},{9,1... | collective-permute-start | bytes 3145736 | tf_op jit(solution)/shard_map/ppermute | solution.py:37
  218.5 3.4 copy-start.2
  221.1 44.5 %collective-permute-start.1 = (bf16[4,32,4096]{2,1,0:T(8,128)(2,1)S(1)}, bf16[4,32,4096]{2,1,0:T(8,128)(2,1)S(1)}, u32[]{:S(2)}, u32[]{:S(2)}) collective-permute-start(bf16[4,32,4096]{2,1,0:T(8,128)(2,1)S(1)} %dynamic-slice_bitcast_fusion.4), channel_id=1, source_target_pairs={{0,2},{2,0},{1,3},{3,1},{4,6},{6,4},{5,7},{7,5},{8,10},{10,8},{9,1... | collective-permute-start | bytes 3145736 | tf_op jit(solution)/shard_map/ppermute | solution.py:37
  221.9 2.3 copy-start.4
  222.8 65.3 %collective-permute-start.13 = (bf16[4,32,4096]{2,1,0:T(8,128)(2,1)S(1)}, bf16[4,32,4096]{2,1,0:T(8,128)(2,1)S(1)}, u32[]{:S(2)}, u32[]{:S(2)}) collective-permute-start(bf16[4,32,4096]{2,1,0:T(8,128)(2,1)S(1)} %dynamic-slice_bitcast_fusion.2), channel_id=1, source_target_pairs={{0,2},{2,0},{1,3},{3,1},{4,6},{6,4},{5,7},{7,5},{8,10},{10,8},{9,1... | collective-permute-start | bytes 3145736 | tf_op jit(solution)/shard_map/ppermute | solution.py:37
  225.1 84.8 %collective-permute-start.7 = (bf16[4,32,4096]{2,1,0:T(8,128)(2,1)S(1)}, bf16[4,32,4096]{2,1,0:T(8,128)(2,1)S(1)}, u32[]{:S(2)}, u32[]{:S(2)}) collective-permute-start(bf16[4,32,4096]{2,1,0:T(8,128)(2,1)S(1)} %dynamic-slice_bitcast_fusion.3), channel_id=1, source_target_pairs={{0,2},{2,0},{1,3},{3,1},{4,6},{6,4},{5,7},{7,5},{8,10},{10,8},{9,1... | collective-permute-start | bytes 3145736 | tf_op jit(solution)/shard_map/ppermute | solution.py:37
  243.5 69.4 %collective-permute-start.22 = (bf16[32,4096]{1,0:T(8,128)(2,1)S(1)}, bf16[32,4096]{1,0:T(8,128)(2,1)S(1)}, u32[]{:S(2)}, u32[]{:S(2)}) collective-permute-start(bf16[32,4096]{1,0:T(8,128)(2,1)S(1)} %get-tuple-element.35), channel_id=1, source_target_pairs={{0,12},{4,0},{8,4},{12,8},{1,13},{5,1},{9,5},{13,9},{2,14},{6,2},{... | collective-permute-start | bytes 786440 | tf_op jit(solution)/shard_map/ppermute | solution.py:44
  246.3 67.6 %collective-permute-start.21 = (bf16[32,4096]{1,0:T(8,128)(2,1)S(1)}, bf16[32,4096]{1,0:T(8,128)(2,1)S(1)}, u32[]{:S(2)}, u32[]{:S(2)}) collective-permute-start(bf16[32,4096]{1,0:T(8,128)(2,1)S(1)} %get-tuple-element.36), channel_id=1, source_target_pairs={{0,8},{4,12},{8,0},{12,4},{1,9},{5,13},{9,1},{13,5},{2,10},{6,14},... | collective-permute-start | bytes 786440 | tf_op jit(solution)/shard_map/ppermute | solution.py:44
  265.7 50.7 %collective-permute-start.20 = (bf16[32,4096]{1,0:T(8,128)(2,1)S(1)}, bf16[32,4096]{1,0:T(8,128)(2,1)S(1)}, u32[]{:S(2)}, u32[]{:S(2)}) collective-permute-start(bf16[32,4096]{1,0:T(8,128)(2,1)S(1)} %get-tuple-element.34), channel_id=1, source_target_pairs={{0,4},{4,8},{8,12},{12,0},{1,5},{5,9},{9,13},{13,1},{2,6},{6,10},{... | collective-permute-start | bytes 786440 | tf_op jit(solution)/shard_map/ppermute | solution.py:44
  288.1 40.9 %copy-start.7 = (f32[1,1,128,4096]{3,2,1,0:T(8,128)S(1)}, f32[1,1,128,4096]{3,2,1,0:T(8,128)}, u32[]{:S(2)}) copy-start(f32[1,1,128,4096]{3,2,1,0:T(8,128)} %convert_element_type.216) | copy-start | bytes 6291460
  288.1 28.3 %collective-permute-start.4 = (bf16[32,4096]{1,0:T(8,128)(2,1)S(1)}, bf16[32,4096]{1,0:T(8,128)(2,1)S(1)}, u32[]{:S(2)}, u32[]{:S(2)}) collective-permute-start(bf16[32,4096]{1,0:T(8,128)(2,1)S(1)} %get-tuple-element.26), channel_id=1, source_target_pairs={{0,12},{4,0},{8,4},{12,8},{1,13},{5,1},{9,5},{13,9},{2,14},{6,2},{... | collective-permute-start | bytes 786440 | tf_op jit(solution)/shard_map/ppermute | solution.py:44
  309.9 10.7 %collective-permute-start.3 = (bf16[32,4096]{1,0:T(8,128)(2,1)S(1)}, bf16[32,4096]{1,0:T(8,128)(2,1)S(1)}, u32[]{:S(2)}, u32[]{:S(2)}) collective-permute-start(bf16[32,4096]{1,0:T(8,128)(2,1)S(1)} %get-tuple-element.27), channel_id=1, source_target_pairs={{0,8},{4,12},{8,0},{12,4},{1,9},{5,13},{9,1},{13,5},{2,10},{6,14},... | collective-permute-start | bytes 786440 | tf_op jit(solution)/shard_map/ppermute | solution.py:44
  313.0 16.0 %collective-permute-start.2 = (bf16[32,4096]{1,0:T(8,128)(2,1)S(1)}, bf16[32,4096]{1,0:T(8,128)(2,1)S(1)}, u32[]{:S(2)}, u32[]{:S(2)}) collective-permute-start(bf16[32,4096]{1,0:T(8,128)(2,1)S(1)} %get-tuple-element.25), channel_id=1, source_target_pairs={{0,4},{4,8},{8,12},{12,0},{1,5},{5,9},{9,13},{13,1},{2,6},{6,10},{... | collective-permute-start | bytes 786440 | tf_op jit(solution)/shard_map/ppermute | solution.py:44
  313.9 15.1 %collective-permute-start.16 = (bf16[32,4096]{1,0:T(8,128)(2,1)S(1)}, bf16[32,4096]{1,0:T(8,128)(2,1)S(1)}, u32[]{:S(2)}, u32[]{:S(2)}) collective-permute-start(bf16[32,4096]{1,0:T(8,128)(2,1)S(1)} %get-tuple-element.32), channel_id=1, source_target_pairs={{0,12},{4,0},{8,4},{12,8},{1,13},{5,1},{9,5},{13,9},{2,14},{6,2},{... | collective-permute-start | bytes 786440 | tf_op jit(solution)/shard_map/ppermute | solution.py:44
  316.3 15.5 %collective-permute-start.15 = (bf16[32,4096]{1,0:T(8,128)(2,1)S(1)}, bf16[32,4096]{1,0:T(8,128)(2,1)S(1)}, u32[]{:S(2)}, u32[]{:S(2)}) collective-permute-start(bf16[32,4096]{1,0:T(8,128)(2,1)S(1)} %get-tuple-element.33), channel_id=1, source_target_pairs={{0,8},{4,12},{8,0},{12,4},{1,9},{5,13},{9,1},{13,5},{2,10},{6,14},... | collective-permute-start | bytes 786440 | tf_op jit(solution)/shard_map/ppermute | solution.py:44
  316.4 23.7 %collective-permute-start.14 = (bf16[32,4096]{1,0:T(8,128)(2,1)S(1)}, bf16[32,4096]{1,0:T(8,128)(2,1)S(1)}, u32[]{:S(2)}, u32[]{:S(2)}) collective-permute-start(bf16[32,4096]{1,0:T(8,128)(2,1)S(1)} %get-tuple-element.31), channel_id=1, source_target_pairs={{0,4},{4,8},{8,12},{12,0},{1,5},{5,9},{9,13},{13,1},{2,6},{6,10},{... | collective-permute-start | bytes 786440 | tf_op jit(solution)/shard_map/ppermute | solution.py:44
  320.6 19.6 %collective-permute-start.10 = (bf16[32,4096]{1,0:T(8,128)(2,1)S(1)}, bf16[32,4096]{1,0:T(8,128)(2,1)S(1)}, u32[]{:S(2)}, u32[]{:S(2)}) collective-permute-start(bf16[32,4096]{1,0:T(8,128)(2,1)S(1)} %get-tuple-element.29), channel_id=1, source_target_pairs={{0,12},{4,0},{8,4},{12,8},{1,13},{5,1},{9,5},{13,9},{2,14},{6,2},{... | collective-permute-start | bytes 786440 | tf_op jit(solution)/shard_map/ppermute | solution.py:44
  329.0 14.1 %collective-permute-start.9 = (bf16[32,4096]{1,0:T(8,128)(2,1)S(1)}, bf16[32,4096]{1,0:T(8,128)(2,1)S(1)}, u32[]{:S(2)}, u32[]{:S(2)}) collective-permute-start(bf16[32,4096]{1,0:T(8,128)(2,1)S(1)} %get-tuple-element.30), channel_id=1, source_target_pairs={{0,8},{4,12},{8,0},{12,4},{1,9},{5,13},{9,1},{13,5},{2,10},{6,14},... | collective-permute-start | bytes 786440 | tf_op jit(solution)/shard_map/ppermute | solution.py:44
  329.0 18.1 %collective-permute-start.8 = (bf16[32,4096]{1,0:T(8,128)(2,1)S(1)}, bf16[32,4096]{1,0:T(8,128)(2,1)S(1)}, u32[]{:S(2)}, u32[]{:S(2)}) collective-permute-start(bf16[32,4096]{1,0:T(8,128)(2,1)S(1)} %get-tuple-element.28), channel_id=1, source_target_pairs={{0,4},{4,8},{8,12},{12,0},{1,5},{5,9},{9,13},{13,1},{2,6},{6,10},{... | collective-permute-start | bytes 786440 | tf_op jit(solution)/shard_map/ppermute | solution.py:44
  331.8 25.8 %collective-permute-start.23 = (bf16[32,4096]{1,0:T(8,128)(2,1)S(1)}, bf16[32,4096]{1,0:T(8,128)(2,1)S(1)}, u32[]{:S(2)}, u32[]{:S(2)}) collective-permute-start(bf16[32,4096]{1,0:T(8,128)(2,1)S(1)} %fusion.91), channel_id=1, source_target_pairs={{48,0},{0,16},{16,32},{32,48},{49,1},{1,17},{17,33},{33,49},{50,2}... | collective-permute-start | bytes 786440 | tf_op jit(solution)/shard_map/ppermute | solution.py:21
  347.6 10.5 %collective-permute-start.17 = (bf16[32,4096]{1,0:T(8,128)(2,1)S(1)}, bf16[32,4096]{1,0:T(8,128)(2,1)S(1)}, u32[]{:S(2)}, u32[]{:S(2)}) collective-permute-start(bf16[32,4096]{1,0:T(8,128)(2,1)S(1)} %get-tuple-element.19), channel_id=1, source_target_pairs={{48,0},{0,16},{16,32},{32,48},{49,1},{1,17},{17,33},{33,49},{50,2}... | collective-permute-start | bytes 786440 | tf_op jit(solution)/shard_map/ppermute | solution.py:21
  349.3 14.5 %collective-permute-start.11 = (bf16[32,4096]{1,0:T(8,128)(2,1)S(1)}, bf16[32,4096]{1,0:T(8,128)(2,1)S(1)}, u32[]{:S(2)}, u32[]{:S(2)}) collective-permute-start(bf16[32,4096]{1,0:T(8,128)(2,1)S(1)} %get-tuple-element.20), channel_id=1, source_target_pairs={{48,0},{0,16},{16,32},{32,48},{49,1},{1,17},{17,33},{33,49},{50,2}... | collective-permute-start | bytes 786440 | tf_op jit(solution)/shard_map/ppermute | solution.py:21
  350.8 17.5 %collective-permute-start.5 = (bf16[32,4096]{1,0:T(8,128)(2,1)S(1)}, bf16[32,4096]{1,0:T(8,128)(2,1)S(1)}, u32[]{:S(2)}, u32[]{:S(2)}) collective-permute-start(bf16[32,4096]{1,0:T(8,128)(2,1)S(1)} %get-tuple-element.18), channel_id=1, source_target_pairs={{48,0},{0,16},{16,32},{32,48},{49,1},{1,17},{17,33},{33,49},{50,2}... | collective-permute-start | bytes 786440 | tf_op jit(solution)/shard_map/ppermute | solution.py:21
  352.1 5.1 %collective-permute-start.24 = (f32[1,3]{1,0:T(1,128)S(1)}, f32[1,3]{1,0:T(1,128)S(1)}, u32[]{:S(2)}, u32[]{:S(2)}) collective-permute-start(f32[1,3]{1,0:T(1,128)S(1)} %maximum_bitcast_fusion.1), channel_id=1, source_target_pairs={{64,0},{0,64},{65,1},{1,65},{66,2},{2,66},{67,3},{3,67},{68,4},{4,... | collective-permute-start | bytes 44 | tf_op jit(solution)/shard_map/ppermute | solution.py:21
Sparse Core Ops, SparseCore 0:
  11.6 94.0 all-gather.1

commit v5 on v3

--- a/solution.py
+++ b/solution.py
@@ -12,7 +12,8 @@
 CHIPS = ("ty", "tx")
 CORE = "tc"
 TENSOR = CHIPS + (CORE,)
-N_BLOCKS = 2
+BLOCK_SPLIT = (56, 48, 24)
+N_BLOCKS = len(BLOCK_SPLIT)
 
 
 def from_behind(block, axis, distance):
@@ -74,17 +75,21 @@
     out_local = out_weight[0]
     n_dev = lax.axis_size(TENSOR)
     local_rows = inputs.shape[0]
-    sub = local_rows // N_BLOCKS
-    block_rows = n_dev * sub
+    bounds = [0]
+    for size in BLOCK_SPLIT:
+        bounds.append(bounds[-1] + size * local_rows // sum(BLOCK_SPLIT))
     col_ids = jnp.arange(seq_len)
     pieces = []
     peaks = []
     for b in range(N_BLOCKS):
+        lo, hi = bounds[b], bounds[b + 1]
+        sub = hi - lo
+        block_rows = n_dev * sub
         query_block = query_heads.reshape(n_dev, local_rows, kv_dev, group_loc, HD)[
-            :, b * sub : (b + 1) * sub
+            :, lo:hi
         ].reshape(block_rows, kv_dev, group_loc, HD)
         row_ids = (
-            jnp.arange(n_dev)[:, None] * local_rows + b * sub + jnp.arange(sub)[None, :]
+            jnp.arange(n_dev)[:, None] * local_rows + lo + jnp.arange(sub)[None, :]
         ).reshape(block_rows)
         scores = (
             jnp.einsum("qkgd,skd->kgqs", query_block, key_heads, preferred_element_type=jnp.float32)
@@ -106,7 +111,7 @@
         peaks.append(jnp.max(row_max[..., 0], axis=2))
         partial = jnp.dot(attended, out_local, preferred_element_type=jnp.float32).astype(jnp.bfloat16)
         summed = scatter_sum(partial)
-        result = (wide_in[b * sub : (b + 1) * sub] + summed).astype(jnp.bfloat16)
+        result = (wide_in[lo:hi] + summed).astype(jnp.bfloat16)
         pieces.append(from_behind(result, "pipe", 1))
     peaks_local = jnp.max(jnp.stack(peaks), axis=0)
     peak_all = jnp.maximum(peaks_local, from_behind(peaks_local, "dp", 1))

time: 390 us -> 383 us (0.982)
  the two profiles are of different devices: /device:TPU:0 before, /device:TPU:2 now
where the time goes in v5:
time: 383 us; the launch traced here: 379 us
  waiting for transfers between devices  168 us (44%)
  matrix products  63.9 us (17%)
  other arithmetic  53.4 us (14%)
  starting transfers between devices  44.6 us (12%)
  local copies, waits for them, and re-layouts  34.2 us (9%)
  between operations  14.7 us (4%)
    all_gather x1, waiting for transfers between devices, on_device_body(): lax.all_gather(normed, TENSOR, axis=0, tiled=True)  83.5 us
    ppermute x21, waiting for transfers between devices, scatter_sum(): got = lax.ppermute(send, CHIPS, route)  74.1 us
    ppermute x21, starting transfers between devices, scatter_sum(): got = lax.ppermute(send, CHIPS, route)  37.3 us
    reduce_max x3, other arithmetic, on_device_body(): peaks.append(jnp.max(row_max[..., 0], axis=2))  21.8 us
    dot_general x3, matrix products, on_device_body(): jnp.einsum('kgqs,skd->qkgd', expw.astype(jnp.bfloat16), value_heads, pref...  19 us
    dot_general x3, matrix products, on_device_body(): jnp.einsum('qkgd,skd->kgqs', query_block, key_heads, preferred_element_ty...  17.7 us
    dot_general x1, matrix products, on_device_body(): jnp.dot(lax.all_gather(normed, TENSOR, axis=0, tiled=True), joined, prefe...  17.4 us
    slice x5, local copies, waits for them, and re-layouts, on_device_body(): query_heads.reshape(n_dev, local_rows, kv_dev, group_loc, HD)[:, lo:hi]  10.5 us
  transfers between devices with their start and end apart: 29, of which 9 were waited for; matrix products, arithmetic and copies ran while one was open for 25% of the time, Pallas kernels for 0%

profile of v5, /device:TPU:2, one launch (start us, length us, event | category | flops | bytes accessed | tf_op | source)
XLA Modules:
  0.0 378.8 jit_solution(9227282404859947799)
XLA Ops:
  7.2 1.7 fusion.37
  8.9 2.5 fusion.39
  12.0 1.5 iota_compare_fusion.2
  13.5 2.5 iota_compare_fusion.1
  16.0 3.1 dynamic-slice_bitcast_fusion.2
  19.1 2.8 iota_compare_fusion
  21.9 83.5 %all-gather.2.cloned.1.call-done = bf16[2048,4096]{1,0:T(8,128)(2,1)} async-done(((bf16[128,4096]{1,0:T(8,128)(2,1)}), bf16[2048,4096]{1,0:T(8,128)(2,1)}) %all-gather.2.cloned.1.call-update) | async-done | bytes 16777232 | tf_op jit(solution)/shard_map/all_gather | solution.py:62
  105.3 17.4 %fusion.30 = bf16[2048,640]{0,1:T(8,128)(2,1)} fusion(bf16[2048,4096]{1,0:T(8,128)(2,1)} %all-gather.2.cloned.1.call-done, bf16[4096,256]{1,0:T(8,128)(2,1)} %dynamic-slice_bitcast_fusion.2, bf16[4096,384]{1,0:T(8,128)(2,1)} %bitcast.303), kind=kOutput, calls=%fused_computation.41 | convolution fusion | flops 10749214720 | bytes 24641536 | tf_op jit(solution)/shard_map/dot_general | solution.py:61
  122.8 2.3 slice.53
  125.1 1.5 slice_bitcast_fusion
  127.0 1.8 slice.61
  128.8 1.7 slice.59
  130.5 2.6 copy.8
  133.1 1.9 copy.14
  135.0 2.6 copy.11
  137.6 3.3 fusion.21
  141.0 3.4 fusion.20
  144.4 2.8 fusion.52
  147.2 1.8 convolution_convert_fusion.2
  149.1 1.4 dynamic-slice_bitcast_fusion.3
  151.2 4.2 %fusion.7 = (f32[3,768]{1,0:T(4,128)S(1)}, f32[2048,768,3]{1,0,2:T(8,128)S(1)}) fusion(pred[768,2048]{0,1:T(8,128)(4,1)S(1)} %copy-done.8, bf16[768,3,128]{2,0,1:T(8,128)(2,1)S(1)} %bitcast.296, bf16[2048,1,2,128]{0,3,2,1:T(8,128)(2,1)S(1)} %bitcast.291), kind=kOutput, calls=%fused_computation.11 | convolution fusion | flops 1222113024 | bytes 21570560 | tf_op jit(solution)/shard_map/qkgd,skd->kgqs/dot_general | solution.py:95
  155.5 6.8 %fusion.6 = (f32[3]{0:T(128)S(1)}, f32[3,768]{1,0:T(4,128)S(1)}) fusion(f32[2048,768,3]{1,0,2:T(8,128)S(1)} %get-tuple-element.32, pred[768,2048]{0,1:T(8,128)(4,1)S(1)} %copy-done.8, f32[3,768]{1,0:T(4,128)S(1)} %get-tuple-element.31), kind=kLoop, calls=%fused_computation.10 | loop fusion | flops 23590652 | bytes 20465676 | tf_op jit(solution)/shard_map/reduce_max | solution.py:111
  162.2 5.5 %divide_convert_fusion.1 = bf16[768,1,3,128]{0,3,2,1:T(8,128)(2,1)S(1)} fusion(f32[2048,768,3]{1,0,2:T(8,128)S(1)} %get-tuple-element.32, f32[3,768]{1,0:T(4,128)S(1)} %get-tuple-element.31, pred[768,2048]{0,1:T(8,128)(4,1)S(1)} %copy-done.8, f32[768,3]{0,1:T(4,128)S(1)} %bitcast.301, bf16[2048,1,2,128]{0,3,2,1:T(8,128)(2,1)S(1)} %bitcast.292), kind=kOutput, calls=%fused_computation.61 | convolution fusion | flops 1227423744 | bytes 21585920 | tf_op jit(solution)/shard_map/kgqs,skd->qkgd/dot_general | solution.py:103
  167.7 3.7 convolution_convert_fusion.1
  171.5 3.0 copy-done.9
  174.5 1.8 dynamic-slice_bitcast_fusion.1
  176.5 10.1 %fusion.5 = (f32[3,896]{1,0:T(4,128)S(1)}, f32[2048,896,3]{1,0,2:T(8,128)}) fusion(pred[896,2048]{0,1:T(8,128)(4,1)S(1)} %copy-done.5, bf16[896,3,128]{2,0,1:T(8,128)(2,1)S(1)} %bitcast.295, bf16[2048,1,2,128]{0,3,2,1:T(8,128)(2,1)S(1)} %bitcast.293), kind=kOutput, calls=%fused_computation.9 | convolution fusion | flops 1425798528 | bytes 25078272 | tf_op jit(solution)/shard_map/qkgd,skd->kgqs/dot_general | solution.py:95
  186.6 11.6 %fusion.4 = (f32[3]{0:T(128)S(1)}, f32[3,896]{1,0:T(4,128)S(1)}) fusion(f32[2048,896,3]{1,0,2:T(8,128)} %get-tuple-element.34, pred[896,2048]{0,1:T(8,128)(4,1)S(1)} %copy-done.5, f32[3,896]{1,0:T(4,128)S(1)} %get-tuple-element.33), kind=kLoop, calls=%fused_computation.8 | loop fusion | flops 27522428 | bytes 23876620 | tf_op jit(solution)/shard_map/reduce_max | solution.py:111
  198.2 10.8 %divide_convert_fusion = bf16[896,1,3,128]{0,3,2,1:T(8,128)(2,1)S(1)} fusion(f32[2048,896,3]{1,0,2:T(8,128)} %get-tuple-element.34, f32[3,896]{1,0:T(4,128)S(1)} %get-tuple-element.33, pred[896,2048]{0,1:T(8,128)(4,1)S(1)} %copy-done.5, f32[896,3]{0,1:T(4,128)S(1)} %bitcast.300, bf16[2048,1,2,128]{0,3,2,1:T(8,128)(2,1)S(1)} %bitcast.294), kind=kOutput, calls=%fused_computation.59 | convolution fusion | flops 1431994368 | bytes 25096192 | tf_op jit(solution)/shard_map/kgqs,skd->qkgd/dot_general | solution.py:103
  209.0 4.2 %convolution_convert_fusion = bf16[896,4096]{1,0:T(8,128)(2,1)S(1)} fusion(bf16[896,384]{0,1:T(8,128)(2,1)S(1)} %bitcast.304, bf16[1,384,4096]{2,1,0:T(8,128)(2,1)S(1)} %copy-done), kind=kOutput, calls=%fused_computation.25 | convolution fusion | flops 2822242304 | bytes 11173888 | tf_op jit(solution)/shard_map/dot_general | solution.py:112
  213.3 2.9 copy-done.6
  216.2 2.3 dynamic-slice_bitcast_fusion
  218.7 2.4 fusion.33
  222.2 1.6 collective-permute-start.19
  224.3 4.2 %fusion.19 = bf16[8,48,4096]{2,1,0:T(8,128)(2,1)S(1)} fusion(bf16[8,48,4096]{2,1,0:T(8,128)(2,1)} %collective-permute-done.9, bf16[8,2,48,4096]{3,2,1,0:T(8,128)(2,1)} %bitcast.288, s32[]{:T(128)S(6)} %select_n.137), kind=kLoop, calls=%fused_computation.28 | loop fusion | flops 6291456 | bytes 9437188 | tf_op jit(solution)/shard_map/convert_element_type | solution.py:33
  229.8 3.0 collective-permute-start.10
  232.8 2.5 collective-permute-start.15
  235.4 3.5 fusion.18
  239.0 2.3 collective-permute-start.14
  241.2 1.8 dynamic-slice_bitcast_fusion.10
  243.0 2.3 collective-permute-start.1
  245.3 1.4 collective-permute-start.7
  246.7 5.5 %collective-permute-done.16 = bf16[48,4096]{1,0:T(8,128)(2,1)} collective-permute-done((bf16[48,4096]{1,0:T(8,128)(2,1)S(1)}, bf16[48,4096]{1,0:T(8,128)(2,1)}, u32[]{:S(2)}, u32[]{:S(2)}) %collective-permute-start.16) | collective-permute-done | bytes 393248 | tf_op jit(solution)/shard_map/ppermute | solution.py:39
  252.2 2.2 collective-permute-start.13
  254.4 24.6 %collective-permute-done.15 = bf16[48,4096]{1,0:T(8,128)(2,1)} collective-permute-done((bf16[48,4096]{1,0:T(8,128)(2,1)S(1)}, bf16[48,4096]{1,0:T(8,128)(2,1)}, u32[]{:S(2)}, u32[]{:S(2)}) %collective-permute-start.15) | collective-permute-done | bytes 393248 | tf_op jit(solution)/shard_map/ppermute | solution.py:39
  279.2 2.8 convert_element_type.165
  282.0 4.0 %collective-permute-start.6 = (bf16[56,4096]{1,0:T(8,128)(2,1)}, bf16[56,4096]{1,0:T(8,128)(2,1)S(1)}, u32[]{:S(2)}, u32[]{:S(2)}) collective-permute-start(bf16[56,4096]{1,0:T(8,128)(2,1)} %get-tuple-element.10), channel_id=1, source_target_pairs={{0,12},{2,14},{4,0},{6,2},{8,4},{10,6},{12,8},{14,10},{1,13},{3,15... | collective-permute-start | bytes 1376264 | tf_op jit(solution)/shard_map/ppermute | solution.py:39
  286.0 3.4 collective-permute-done.12
  289.4 2.6 collective-permute-start.5
  292.0 22.5 %collective-permute-done.11 = bf16[48,4096]{1,0:T(8,128)(2,1)} collective-permute-done((bf16[48,4096]{1,0:T(8,128)(2,1)}, bf16[48,4096]{1,0:T(8,128)(2,1)}, u32[]{:S(2)}, u32[]{:S(2)}) %collective-permute-start.11) | collective-permute-done | bytes 393248 | tf_op jit(solution)/shard_map/ppermute | solution.py:39
  315.9 1.9 collective-permute-start.2
  317.8 2.4 fusion.68
  320.2 1.4 collective-permute-start.24
  321.7 6.0 %collective-permute-start.23 = (bf16[24,4096]{1,0:T(8,128)(2,1)}, bf16[24,4096]{1,0:T(8,128)(2,1)S(1)}, u32[]{:S(2)}, u32[]{:S(2)}) collective-permute-start(bf16[24,4096]{1,0:T(8,128)(2,1)} %get-tuple-element.25), channel_id=1, source_target_pairs={{0,10},{2,12},{4,14},{6,0},{8,2},{10,4},{12,6},{14,8},{1,11},{3,13... | collective-permute-start | bytes 589832 | tf_op jit(solution)/shard_map/ppermute | solution.py:39
  327.6 12.0 %collective-permute-done.4 = bf16[56,4096]{1,0:T(8,128)(2,1)S(1)} collective-permute-done((bf16[56,4096]{1,0:T(8,128)(2,1)}, bf16[56,4096]{1,0:T(8,128)(2,1)S(1)}, u32[]{:S(2)}, u32[]{:S(2)}) %collective-permute-start.4) | collective-permute-done | bytes 458784 | tf_op jit(solution)/shard_map/ppermute | solution.py:39
  339.6 1.8 collective-permute-start.22
  341.5 5.9 %collective-permute-done.2 = bf16[56,4096]{1,0:T(8,128)(2,1)S(1)} collective-permute-done((bf16[56,4096]{1,0:T(8,128)(2,1)}, bf16[56,4096]{1,0:T(8,128)(2,1)S(1)}, u32[]{:S(2)}, u32[]{:S(2)}) %collective-permute-start.2) | collective-permute-done | bytes 458784 | tf_op jit(solution)/shard_map/ppermute | solution.py:39
  347.4 2.4 collective-permute-start.20
  349.8 2.1 fusion.56
  351.9 1.6 collective-permute-start.17
  353.6 1.6 collective-permute-start.8
  357.9 1.9 collective-permute-start.27
  359.8 3.2 collective-permute-done.27
  363.4 7.2 %collective-permute-done.26 = bf16[24,4096]{1,0:T(8,128)(2,1)S(1)} collective-permute-done((bf16[24,4096]{1,0:T(8,128)(2,1)S(1)}, bf16[24,4096]{1,0:T(8,128)(2,1)S(1)}, u32[]{:S(2)}, u32[]{:S(2)}) %collective-permute-start.26) | collective-permute-done | bytes 196640 | tf_op jit(solution)/shard_map/ppermute | solution.py:22
  (89 shorter events, 10.7 us)
Async XLA Ops:
  7.2 140.0 %copy-start = (bf16[1,384,4096]{2,1,0:T(8,128)(2,1)S(1)}, bf16[1,384,4096]{2,1,0:T(8,128)(2,1)}, u32[]{:S(2)}) copy-start(bf16[1,384,4096]{2,1,0:T(8,128)(2,1)} %param.9) | copy-start | bytes 9437188
  7.2 98.2 %all-gather.2.cloned.1.call-start = ((), (), s32[]{:S(2)}) async-start(), calls=%async_computation | async-start | bytes 17825792 | tf_op jit(solution)/shard_map/all_gather | solution.py:62
  127.0 1.8 copy-start.1
  137.6 3.4 copy-start.10
  140.9 3.5 copy-start.11
  147.2 4.0 %copy-start.8 = (pred[768,2048]{0,1:T(8,128)(4,1)S(1)}, pred[768,2048]{0,1:T(8,128)(4,1)}, u32[]{:S(2)}) copy-start(pred[768,2048]{0,1:T(8,128)(4,1)} %iota_compare_fusion.1) | copy-start | bytes 4718596
  147.2 4.0 %copy-start.13 = (bf16[16,48,1,3,128]{4,1,0,3,2:T(8,128)(2,1)S(1)}, bf16[16,48,1,3,128]{4,1,0,3,2:T(8,128)(2,1)}, u32[]{:S(2)}) copy-start(bf16[16,48,1,3,128]{4,1,0,3,2:T(8,128)(2,1)} %copy.11) | copy-start | bytes 1769476
  149.0 2.2 copy-start.3
  150.4 68.3 %collective-permute-start.18 = (bf16[8,24,4096]{2,1,0:T(8,128)(2,1)}, bf16[8,24,4096]{2,1,0:T(8,128)(2,1)}, u32[]{:S(2)}, u32[]{:S(2)}) collective-permute-start(bf16[8,24,4096]{2,1,0:T(8,128)(2,1)} %dynamic-slice_bitcast_fusion.3), channel_id=1, source_target_pairs={{0,1},{1,0},{2,3},{3,2},{4,5},{5,4},{6,7},{7,6},{8,9},{9,8},{10,11... | collective-permute-start | bytes 4718600 | tf_op jit(solution)/shard_map/ppermute | solution.py:32
  171.4 3.0 copy-start.9
  171.5 5.1 %copy-start.5 = (pred[896,2048]{0,1:T(8,128)(4,1)S(1)}, pred[896,2048]{0,1:T(8,128)(4,1)}, u32[]{:S(2)}) copy-start(pred[896,2048]{0,1:T(8,128)(4,1)} %iota_compare_fusion) | copy-start | bytes 5505028
  171.5 5.1 %copy-start.12 = (bf16[16,56,1,3,128]{4,1,0,3,2:T(8,128)(2,1)S(1)}, bf16[16,56,1,3,128]{4,1,0,3,2:T(8,128)(2,1)}, u32[]{:S(2)}) copy-start(bf16[16,56,1,3,128]{4,1,0,3,2:T(8,128)(2,1)} %copy.8) | copy-start | bytes 2064388
  176.3 48.0 %collective-permute-start.9 = (bf16[8,48,4096]{2,1,0:T(8,128)(2,1)}, bf16[8,48,4096]{2,1,0:T(8,128)(2,1)}, u32[]{:S(2)}, u32[]{:S(2)}) collective-permute-start(bf16[8,48,4096]{2,1,0:T(8,128)(2,1)} %dynamic-slice_bitcast_fusion.1), channel_id=1, source_target_pairs={{0,1},{1,0},{2,3},{3,2},{4,5},{5,4},{6,7},{7,6},{8,9},{9,8},{10,11... | collective-permute-start | bytes 9437192 | tf_op jit(solution)/shard_map/ppermute | solution.py:32
  213.3 2.9 copy-start.6
  218.5 14.4 %collective-permute-start = (bf16[8,56,4096]{2,1,0:T(8,128)(2,1)}, bf16[8,56,4096]{2,1,0:T(8,128)(2,1)}, u32[]{:S(2)}, u32[]{:S(2)}) collective-permute-start(bf16[8,56,4096]{2,1,0:T(8,128)(2,1)} %dynamic-slice_bitcast_fusion), channel_id=1, source_target_pairs={{0,1},{1,0},{2,3},{3,2},{4,5},{5,4},{6,7},{7,6},{8,9},{9,8},{10,11... | collective-permute-start | bytes 11010056 | tf_op jit(solution)/shard_map/ppermute | solution.py:32
  221.2 3.1 copy-start.7
  222.2 16.7 %collective-permute-start.19 = (bf16[24,4096]{1,0:T(8,128)(2,1)S(1)}, bf16[24,4096]{1,0:T(8,128)(2,1)S(1)}, u32[]{:S(2)}, u32[]{:S(2)}) collective-permute-start(bf16[24,4096]{1,0:T(8,128)(2,1)S(1)} %get-tuple-element.22), channel_id=1, source_target_pairs={{0,2},{2,4},{4,6},{6,8},{8,10},{10,12},{12,14},{14,0},{1,3},{3,5},... | collective-permute-start | bytes 589832 | tf_op jit(solution)/shard_map/ppermute | solution.py:39
  223.9 11.5 %slice-start = ((s8[7340032]{0:T(1024)(128)(4,1)}), s8[4194304]{0:T(1024)(128)(4,1)S(1)}, s32[]{:S(2)}) async-start(s8[7340032]{0:T(1024)(128)(4,1)} %bitcast.284), calls=%async_computation.1 | async-start | bytes 8388608
  223.9 11.5 %slice-start.1 = ((s8[7340032]{0:T(1024)(128)(4,1)}), s8[3145728]{0:T(1024)(128)(4,1)S(1)}, s32[]{:S(2)}) async-start(s8[7340032]{0:T(1024)(128)(4,1)} %bitcast.284), calls=%async_computation.2 | async-start | bytes 6291456
  223.9 19.1 %collective-permute-start.25 = (bf16[24,4096]{1,0:T(8,128)(2,1)S(1)}, bf16[24,4096]{1,0:T(8,128)(2,1)S(1)}, u32[]{:S(2)}, u32[]{:S(2)}) collective-permute-start(bf16[24,4096]{1,0:T(8,128)(2,1)S(1)} %get-tuple-element.23), channel_id=1, source_target_pairs={{0,14},{2,0},{4,2},{6,4},{8,6},{10,8},{12,10},{14,12},{1,15},{3,1}... | collective-permute-start | bytes 589832 | tf_op jit(solution)/shard_map/ppermute | solution.py:39
  228.5 4.3 %copy-start.4 = (bf16[8,48,4096]{2,1,0:T(8,128)(2,1)}, bf16[8,48,4096]{2,1,0:T(8,128)(2,1)S(1)}, u32[]{:S(2)}) copy-start(bf16[8,48,4096]{2,1,0:T(8,128)(2,1)S(1)} %fusion.19) | copy-start | bytes 9437188
  229.8 15.4 %collective-permute-start.10 = (bf16[48,4096]{1,0:T(8,128)(2,1)S(1)}, bf16[48,4096]{1,0:T(8,128)(2,1)S(1)}, u32[]{:S(2)}, u32[]{:S(2)}) collective-permute-start(bf16[48,4096]{1,0:T(8,128)(2,1)S(1)} %get-tuple-element.15), channel_id=1, source_target_pairs={{0,2},{2,4},{4,6},{6,8},{8,10},{10,12},{12,14},{14,0},{1,3},{3,5},... | collective-permute-start | bytes 1179656 | tf_op jit(solution)/shard_map/ppermute | solution.py:39
  232.8 19.4 %collective-permute-start.16 = (bf16[48,4096]{1,0:T(8,128)(2,1)S(1)}, bf16[48,4096]{1,0:T(8,128)(2,1)}, u32[]{:S(2)}, u32[]{:S(2)}) collective-permute-start(bf16[48,4096]{1,0:T(8,128)(2,1)S(1)} %get-tuple-element.16), channel_id=1, source_target_pairs={{0,14},{2,0},{4,2},{6,4},{8,6},{10,8},{12,10},{14,12},{1,15},{3,1}... | collective-permute-start | bytes 1179656 | tf_op jit(solution)/shard_map/ppermute | solution.py:39
  232.8 46.2 %collective-permute-start.15 = (bf16[48,4096]{1,0:T(8,128)(2,1)S(1)}, bf16[48,4096]{1,0:T(8,128)(2,1)}, u32[]{:S(2)}, u32[]{:S(2)}) collective-permute-start(bf16[48,4096]{1,0:T(8,128)(2,1)S(1)} %get-tuple-element.17), channel_id=1, source_target_pairs={{0,12},{2,14},{4,0},{6,2},{8,4},{10,6},{12,8},{14,10},{1,13},{3,15... | collective-permute-start | bytes 1179656 | tf_op jit(solution)/shard_map/ppermute | solution.py:39
  238.9 2.3 copy-start.2
  239.0 40.1 %copy-start.14 = (bf16[24,4096]{1,0:T(8,128)(2,1)}, bf16[24,4096]{1,0:T(8,128)(2,1)S(1)}, u32[]{:S(2)}) copy-start(bf16[24,4096]{1,0:T(8,128)(2,1)S(1)} %collective-permute-done.19) | copy-start | bytes 589828
  239.0 40.1 %collective-permute-start.14 = (bf16[48,4096]{1,0:T(8,128)(2,1)S(1)}, bf16[48,4096]{1,0:T(8,128)(2,1)}, u32[]{:S(2)}, u32[]{:S(2)}) collective-permute-start(bf16[48,4096]{1,0:T(8,128)(2,1)S(1)} %get-tuple-element.18), channel_id=1, source_target_pairs={{0,10},{2,12},{4,14},{6,0},{8,2},{10,4},{12,6},{14,8},{1,11},{3,13... | collective-permute-start | bytes 1179656 | tf_op jit(solution)/shard_map/ppermute | solution.py:39
  243.0 36.1 %copy-start.16 = (bf16[24,4096]{1,0:T(8,128)(2,1)}, bf16[24,4096]{1,0:T(8,128)(2,1)S(1)}, u32[]{:S(2)}) copy-start(bf16[24,4096]{1,0:T(8,128)(2,1)S(1)} %collective-permute-done.25) | copy-start | bytes 589828
  243.0 72.9 %collective-permute-start.1 = (bf16[56,4096]{1,0:T(8,128)(2,1)}, bf16[56,4096]{1,0:T(8,128)(2,1)}, u32[]{:S(2)}, u32[]{:S(2)}) collective-permute-start(bf16[56,4096]{1,0:T(8,128)(2,1)} %get-tuple-element.8), channel_id=1, source_target_pairs={{0,2},{2,4},{4,6},{6,8},{8,10},{10,12},{12,14},{14,0},{1,3},{3,5},... | collective-permute-start | bytes 1376264 | tf_op jit(solution)/shard_map/ppermute | solution.py:39
  245.3 70.6 %collective-permute-start.7 = (bf16[56,4096]{1,0:T(8,128)(2,1)}, bf16[56,4096]{1,0:T(8,128)(2,1)}, u32[]{:S(2)}, u32[]{:S(2)}) collective-permute-start(bf16[56,4096]{1,0:T(8,128)(2,1)} %get-tuple-element.9), channel_id=1, source_target_pairs={{0,14},{2,0},{4,2},{6,4},{8,6},{10,8},{12,10},{14,12},{1,15},{3,1}... | collective-permute-start | bytes 1376264 | tf_op jit(solution)/shard_map/ppermute | solution.py:39
  252.2 29.8 %collective-permute-start.13 = (bf16[48,4096]{1,0:T(8,128)(2,1)}, bf16[48,4096]{1,0:T(8,128)(2,1)}, u32[]{:S(2)}, u32[]{:S(2)}) collective-permute-start(bf16[48,4096]{1,0:T(8,128)(2,1)} %get-tuple-element.19), channel_id=1, source_target_pairs={{0,8},{2,10},{4,12},{6,14},{8,0},{10,2},{12,4},{14,6},{1,9},{3,11}... | collective-permute-start | bytes 1179656 | tf_op jit(solution)/shard_map/ppermute | solution.py:39
  279.1 10.3 %collective-permute-start.12 = (bf16[48,4096]{1,0:T(8,128)(2,1)}, bf16[48,4096]{1,0:T(8,128)(2,1)}, u32[]{:S(2)}, u32[]{:S(2)}) collective-permute-start(bf16[48,4096]{1,0:T(8,128)(2,1)} %get-tuple-element.20), channel_id=1, source_target_pairs={{0,6},{2,8},{4,10},{6,12},{8,14},{10,0},{12,2},{14,4},{1,7},{3,9},... | collective-permute-start | bytes 1179656 | tf_op jit(solution)/shard_map/ppermute | solution.py:39
  279.1 35.4 %collective-permute-start.11 = (bf16[48,4096]{1,0:T(8,128)(2,1)}, bf16[48,4096]{1,0:T(8,128)(2,1)}, u32[]{:S(2)}, u32[]{:S(2)}) collective-permute-start(bf16[48,4096]{1,0:T(8,128)(2,1)} %get-tuple-element.21), channel_id=1, source_target_pairs={{0,4},{2,6},{4,8},{6,10},{8,12},{10,14},{12,0},{14,2},{1,5},{3,7},... | collective-permute-start | bytes 1179656 | tf_op jit(solution)/shard_map/ppermute | solution.py:39
  282.0 73.3 %copy-start.15 = (bf16[24,4096]{1,0:T(8,128)(2,1)S(1)}, bf16[24,4096]{1,0:T(8,128)(2,1)}, u32[]{:S(2)}) copy-start(bf16[24,4096]{1,0:T(8,128)(2,1)} %copy-done.14) | copy-start | bytes 589828
  282.0 73.3 %copy-start.17 = (bf16[24,4096]{1,0:T(8,128)(2,1)S(1)}, bf16[24,4096]{1,0:T(8,128)(2,1)}, u32[]{:S(2)}) copy-start(bf16[24,4096]{1,0:T(8,128)(2,1)} %copy-done.16) | copy-start | bytes 589828
  282.0 38.2 %collective-permute-start.6 = (bf16[56,4096]{1,0:T(8,128)(2,1)}, bf16[56,4096]{1,0:T(8,128)(2,1)S(1)}, u32[]{:S(2)}, u32[]{:S(2)}) collective-permute-start(bf16[56,4096]{1,0:T(8,128)(2,1)} %get-tuple-element.10), channel_id=1, source_target_pairs={{0,12},{2,14},{4,0},{6,2},{8,4},{10,6},{12,8},{14,10},{1,13},{3,15... | collective-permute-start | bytes 1376264 | tf_op jit(solution)/shard_map/ppermute | solution.py:39
  289.4 32.3 %collective-permute-start.5 = (bf16[56,4096]{1,0:T(8,128)(2,1)}, bf16[56,4096]{1,0:T(8,128)(2,1)S(1)}, u32[]{:S(2)}, u32[]{:S(2)}) collective-permute-start(bf16[56,4096]{1,0:T(8,128)(2,1)} %get-tuple-element.11), channel_id=1, source_target_pairs={{0,10},{2,12},{4,14},{6,0},{8,2},{10,4},{12,6},{14,8},{1,11},{3,13... | collective-permute-start | bytes 1376264 | tf_op jit(solution)/shard_map/ppermute | solution.py:39
  314.5 25.1 %collective-permute-start.4 = (bf16[56,4096]{1,0:T(8,128)(2,1)}, bf16[56,4096]{1,0:T(8,128)(2,1)S(1)}, u32[]{:S(2)}, u32[]{:S(2)}) collective-permute-start(bf16[56,4096]{1,0:T(8,128)(2,1)} %get-tuple-element.12), channel_id=1, source_target_pairs={{0,8},{2,10},{4,12},{6,14},{8,0},{10,2},{12,4},{14,6},{1,9},{3,11}... | collective-permute-start | bytes 1376264 | tf_op jit(solution)/shard_map/ppermute | solution.py:39
  315.9 25.6 %collective-permute-start.3 = (bf16[56,4096]{1,0:T(8,128)(2,1)}, bf16[56,4096]{1,0:T(8,128)(2,1)S(1)}, u32[]{:S(2)}, u32[]{:S(2)}) collective-permute-start(bf16[56,4096]{1,0:T(8,128)(2,1)} %get-tuple-element.13), channel_id=1, source_target_pairs={{0,6},{2,8},{4,10},{6,12},{8,14},{10,0},{12,2},{14,4},{1,7},{3,9},... | collective-permute-start | bytes 1376264 | tf_op jit(solution)/shard_map/ppermute | solution.py:39
  315.9 31.6 %collective-permute-start.2 = (bf16[56,4096]{1,0:T(8,128)(2,1)}, bf16[56,4096]{1,0:T(8,128)(2,1)S(1)}, u32[]{:S(2)}, u32[]{:S(2)}) collective-permute-start(bf16[56,4096]{1,0:T(8,128)(2,1)} %get-tuple-element.14), channel_id=1, source_target_pairs={{0,4},{2,6},{4,8},{6,10},{8,12},{10,14},{12,0},{14,2},{1,5},{3,7},... | collective-permute-start | bytes 1376264 | tf_op jit(solution)/shard_map/ppermute | solution.py:39
  320.2 31.7 %collective-permute-start.24 = (bf16[24,4096]{1,0:T(8,128)(2,1)}, bf16[24,4096]{1,0:T(8,128)(2,1)S(1)}, u32[]{:S(2)}, u32[]{:S(2)}) collective-permute-start(bf16[24,4096]{1,0:T(8,128)(2,1)} %get-tuple-element.24), channel_id=1, source_target_pairs={{0,12},{2,14},{4,0},{6,2},{8,4},{10,6},{12,8},{14,10},{1,13},{3,15... | collective-permute-start | bytes 589832 | tf_op jit(solution)/shard_map/ppermute | solution.py:39
  321.7 31.9 %collective-permute-start.23 = (bf16[24,4096]{1,0:T(8,128)(2,1)}, bf16[24,4096]{1,0:T(8,128)(2,1)S(1)}, u32[]{:S(2)}, u32[]{:S(2)}) collective-permute-start(bf16[24,4096]{1,0:T(8,128)(2,1)} %get-tuple-element.25), channel_id=1, source_target_pairs={{0,10},{2,12},{4,14},{6,0},{8,2},{10,4},{12,6},{14,8},{1,11},{3,13... | collective-permute-start | bytes 589832 | tf_op jit(solution)/shard_map/ppermute | solution.py:39
  339.6 15.6 %collective-permute-start.22 = (bf16[24,4096]{1,0:T(8,128)(2,1)}, bf16[24,4096]{1,0:T(8,128)(2,1)S(1)}, u32[]{:S(2)}, u32[]{:S(2)}) collective-permute-start(bf16[24,4096]{1,0:T(8,128)(2,1)} %get-tuple-element.26), channel_id=1, source_target_pairs={{0,8},{2,10},{4,12},{6,14},{8,0},{10,2},{12,4},{14,6},{1,9},{3,11}... | collective-permute-start | bytes 589832 | tf_op jit(solution)/shard_map/ppermute | solution.py:39
  341.5 13.7 %collective-permute-start.21 = (bf16[24,4096]{1,0:T(8,128)(2,1)}, bf16[24,4096]{1,0:T(8,128)(2,1)S(1)}, u32[]{:S(2)}, u32[]{:S(2)}) collective-permute-start(bf16[24,4096]{1,0:T(8,128)(2,1)} %get-tuple-element.27), channel_id=1, source_target_pairs={{0,6},{2,8},{4,10},{6,12},{8,14},{10,0},{12,2},{14,4},{1,7},{3,9},... | collective-permute-start | bytes 589832 | tf_op jit(solution)/shard_map/ppermute | solution.py:39
  347.4 7.8 %collective-permute-start.20 = (bf16[24,4096]{1,0:T(8,128)(2,1)}, bf16[24,4096]{1,0:T(8,128)(2,1)S(1)}, u32[]{:S(2)}, u32[]{:S(2)}) collective-permute-start(bf16[24,4096]{1,0:T(8,128)(2,1)} %get-tuple-element.28), channel_id=1, source_target_pairs={{0,4},{2,6},{4,8},{6,10},{8,12},{10,14},{12,0},{14,2},{1,5},{3,7},... | collective-permute-start | bytes 589832 | tf_op jit(solution)/shard_map/ppermute | solution.py:39
  351.9 18.7 %collective-permute-start.17 = (bf16[48,4096]{1,0:T(8,128)(2,1)S(1)}, bf16[48,4096]{1,0:T(8,128)(2,1)S(1)}, u32[]{:S(2)}, u32[]{:S(2)}) collective-permute-start(bf16[48,4096]{1,0:T(8,128)(2,1)S(1)} %fusion.68), channel_id=1, source_target_pairs={{48,0},{0,16},{16,32},{32,48},{49,1},{1,17},{17,33},{33,49},{50,2}... | collective-permute-start | bytes 1179656 | tf_op jit(solution)/shard_map/ppermute | solution.py:22
  353.6 17.1 %collective-permute-start.8 = (bf16[56,4096]{1,0:T(8,128)(2,1)S(1)}, bf16[56,4096]{1,0:T(8,128)(2,1)S(1)}, u32[]{:S(2)}, u32[]{:S(2)}) collective-permute-start(bf16[56,4096]{1,0:T(8,128)(2,1)S(1)} %fusion.56), channel_id=1, source_target_pairs={{48,0},{0,16},{16,32},{32,48},{49,1},{1,17},{17,33},{33,49},{50,2}... | collective-permute-start | bytes 1376264 | tf_op jit(solution)/shard_map/ppermute | solution.py:22
  356.5 14.1 %collective-permute-start.26 = (bf16[24,4096]{1,0:T(8,128)(2,1)S(1)}, bf16[24,4096]{1,0:T(8,128)(2,1)S(1)}, u32[]{:S(2)}, u32[]{:S(2)}) collective-permute-start(bf16[24,4096]{1,0:T(8,128)(2,1)S(1)} %fusion.79), channel_id=1, source_target_pairs={{48,0},{0,16},{16,32},{32,48},{49,1},{1,17},{17,33},{33,49},{50,2}... | collective-permute-start | bytes 589832 | tf_op jit(solution)/shard_map/ppermute | solution.py:22
  357.9 5.1 %collective-permute-start.27 = (f32[1,3]{1,0:T(1,128)S(1)}, f32[1,3]{1,0:T(1,128)S(1)}, u32[]{:S(2)}, u32[]{:S(2)}) collective-permute-start(f32[1,3]{1,0:T(1,128)S(1)} %maximum_bitcast_fusion.1), channel_id=1, source_target_pairs={{64,0},{0,64},{65,1},{1,65},{66,2},{2,66},{67,3},{3,67},{68,4},{4,... | collective-permute-start | bytes 44 | tf_op jit(solution)/shard_map/ppermute | solution.py:22
Sparse Core Ops, SparseCore 0:
  11.6 93.7 all-gather.1
